TPU v7x, 256 devices: a whole 4x4x8 slice. The times are simulated.
256 devices in a mesh: tm: 16 (over y, x), space: 16 (over z, core).
Axes of the slice: x: 4, y: 4, z: 8, core: 2. Of those that a mesh axis runs over, the one named last changes fastest.
Arguments:
- stored: bfloat16 [16, 288, 128, 128], P('tm', None, 'space'), may hold values from -6 to 6
- snapshot: int32 [16, 256], P('tm'), may hold values from 0 to 287, as said below
- balance_coef: float32 [128, 128], P('space'), may hold values from 0.5 to 2
- sea_mask: int32 [128, 128], P('space'), may hold values 0 or 1
Outputs:
- merged_basis: bfloat16 [256, 3, 128, 128], P('tm', None, 'space')
Inputs may be any that keep to these rules, and one draw needn't show every extreme that they name: `snapshot`: the 256 indices of one group are distinct.
All inputs are finite; a program needn't handle non-finite values. No bound on the sum of `sea_mask` on one device may be relied on, other than what follows from the above.
Results may differ from a plain program's by a relative error of at most 0.04.
Values may be sent and summed in bfloat16 or wider, within the bound.
No kernel may reach another device: no remote copies, remote signals or barrier semaphores. Data moves between devices by JAX's collectives and lax.ppermute only.
A program may use at most 64 MiB of HBM per device.

v0:
```python
import jax
import jax.numpy as jnp
from jax import lax
from jax.sharding import PartitionSpec as P

inv_root2 = 0.7071067811865476


def gathered_total(shard, axis):
    return lax.all_gather(shard, axis).astype(jnp.float32).sum(0)


def summed_rows(shard, axis):
    count = lax.axis_size(axis)
    parts = lax.all_to_all(shard, axis, 0, 0, tiled=True)
    parts = parts.reshape(count, shard.shape[0] // count, shard.shape[1])
    own_rows = parts.astype(jnp.float32).sum(0)
    return lax.all_gather(own_rows, axis, axis=0, tiled=True)


def with_halo(cells, sides, width):
    for axis, dim in sides:
        count = lax.axis_size(axis)
        ends = count - 1
        head = lax.slice_in_dim(cells, 0, width, axis=dim)
        tail = lax.slice_in_dim(cells, cells.shape[dim] - width, cells.shape[dim], axis=dim)
        cells = jnp.concatenate(
            [
                lax.ppermute(tail, axis, [(i, (i + 1) % count) for i in range(ends)]),
                cells,
                lax.ppermute(head, axis, [((i + 1) % count, i) for i in range(ends)]),
            ],
            axis=dim,
        )
    return cells


def from_partner(shard, axis, stride):
    return lax.ppermute(shard, axis, [(i, i ^ 1 << stride) for i in range(lax.axis_size(axis))])


def balance(padded, balance_coef, sea_float):
    center = padded[:, 1:-1, :]
    cells = lax.broadcasted_iota(jnp.int32, (center.shape[2], center.shape[2]), 0)
    targets = lax.broadcasted_iota(jnp.int32, (center.shape[2], center.shape[2]), 1)
    count = center.shape[2]
    circulant = (cells == (targets + 1) % count).astype(jnp.bfloat16) - (
        cells == (targets - 1) % count
    ).astype(jnp.bfloat16)
    east_minus_west = jnp.einsum(
        "mxy,yz->mxz", center, circulant, preferred_element_type=jnp.float32
    )
    zonal_flow = (-balance_coef * sea_float * east_minus_west).astype(jnp.bfloat16)
    wide = padded.astype(jnp.float32)
    merid_flow = (balance_coef * sea_float * (wide[:, 2:, :] - wide[:, :-2, :])).astype(
        jnp.bfloat16
    )
    return jnp.stack([center, zonal_flow, merid_flow], axis=1).reshape(center.shape[0], -1)


def stack_pair(own_basis, other_basis):
    return jnp.concatenate([own_basis, other_basis], axis=0)


def rotation_of(stacked):
    members = stacked.shape[0] // 2
    local_gram = jnp.dot(stacked, stacked.T, preferred_element_type=jnp.float32)
    local_mixed = (local_gram[:, :members] + local_gram[:, members:]) * inv_root2
    mixed_cols = summed_rows(local_mixed.astype(jnp.bfloat16), "space")
    normal = jnp.dot(
        mixed_cols.T,
        mixed_cols,
        precision=lax.Precision.HIGHEST,
        preferred_element_type=jnp.float32,
    )
    half = normal.shape[0] // 2
    low_11 = jnp.linalg.cholesky(normal[:half, :half])
    low_21 = lax.linalg.triangular_solve(
        low_11, normal[half:, :half], left_side=False, lower=True, transpose_a=True
    )
    low_22 = jnp.linalg.cholesky(normal[half:, half:] - highest_dot(low_21, low_21.T))
    upper_rows = jax.scipy.linalg.solve_triangular(low_11, mixed_cols[:, :half].T, lower=True)
    lower_rows = jax.scipy.linalg.solve_triangular(
        low_22, mixed_cols[:, half:].T - highest_dot(low_21, upper_rows), lower=True
    )
    return (jnp.concatenate([upper_rows, lower_rows], axis=0) * inv_root2).astype(jnp.bfloat16)


def highest_dot(left, right):
    return jnp.dot(
        left, right, precision=lax.Precision.HIGHEST, preferred_element_type=jnp.float32
    )


def rotated(rotation, stacked):
    return jnp.dot(rotation, stacked, preferred_element_type=jnp.float32).astype(jnp.bfloat16)


def body(stored, snapshot, balance_coef, sea_mask):
    sea_float = sea_mask.astype(jnp.float32)
    mean_state = jnp.mean(stored[0].astype(jnp.float32), axis=0)
    picked = jnp.take(stored[0], snapshot[0], axis=0)
    anomaly = ((picked.astype(jnp.float32) - mean_state) * sea_float).astype(jnp.bfloat16)
    padded = with_halo(anomaly, (("space", 1),), 1)
    basis_now = balance(padded, balance_coef, sea_float)
    levels = lax.axis_size("tm").bit_length() - 1
    other_padded = from_partner(padded, "tm", 0)
    partner = balance(other_padded, balance_coef, sea_float)
    stacked = stack_pair(basis_now, partner)
    for level_idx in range(levels):
        if level_idx == levels - 1:
            rotation = rotation_of(stacked)
            member_share = rotation.shape[0] // lax.axis_size("tm")
            rotation = lax.dynamic_slice_in_dim(
                rotation, lax.axis_index("tm") * member_share, member_share, 0
            )
            basis_now = rotated(rotation, stacked)
        else:
            partner_stacked = from_partner(stacked, "tm", level_idx + 1)
            rotation = rotation_of(stacked)
            partner_rotation = from_partner(rotation, "tm", level_idx + 1)
            basis_now = rotated(rotation, stacked)
            partner = rotated(partner_rotation, partner_stacked)
            stacked = stack_pair(basis_now, partner)
    return basis_now.reshape(basis_now.shape[0], 3, stored.shape[2], stored.shape[3])


def solution(mesh):
    placed = (P("tm", None, "space", None), P("tm", None), P("space", None), P("space", None))
    return jax.shard_map(
        body, mesh=mesh, in_specs=placed, out_specs=P("tm", None, "space", None), check_vma=False
    )
```

profile of v0, /device:TPU:1, one launch (start us, length us, event | category | flops | bytes accessed | tf_op | source)
XLA Modules:
  0.0 418.7 jit_solution(4439654136984365832)
XLA Ops:
  18.8 12.5 %collective-permute-done.2 = bf16[256,10,128]{0,2,1:T(8,128)(2,1)S(1)} collective-permute-done((bf16[256,10,128]{0,2,1:T(8,128)(2,1)S(1)}, bf16[256,10,128]{0,2,1:T(8,128)(2,1)S(1)}, u32[]{:S(2)}, u32[]{:S(2)}) %collective-permute-start.2) | collective-permute-done | bytes 655392 | tf_op jit(solution)/shard_map/ppermute | solution.py:39
  35.2 10.2 %all-to-all-start = ((bf16[16,32,256]{2,1,0:T(8,128)(2,1)}), bf16[16,32,256]{2,1,0:T(8,128)(2,1)S(1)}, u32[]{:S(2)}, u32[]{:S(2)}) async-start(bf16[16,32,256]{2,1,0:T(8,128)(2,1)} %bitcast.13), calls=%async_computation | async-start | bytes 524288 | tf_op jit(solution)/shard_map/all_to_all | solution.py:15
  57.1 16.4 %all_gather.12 = f32[512,256]{1,0:T(8,128)S(1)} all-gather(f32[32,256]{1,0:T(8,128)S(1)} %convert_reduce_fusion.4), channel_id=1, replica_groups=mesh['tm'=16,'space'=16] {'space'}, dimensions={0}, use_global_device_ids=true | all-gather | bytes 557056 | tf_op jit(solution)/shard_map/all_gather | solution.py:18
  74.7 11.7 %cholesky.134 = f32[128,128]{1,0:T(8,128)S(1)} custom-call(f32[128,128]{1,0:T(8,128)S(1)} %get-tuple-element.19), custom_call_target="Cholesky" | custom-call | tf_op jit(solution)/shard_map/jit(cholesky)/cholesky | solution.py:77
  87.8 9.8 %custom-call.18 = f32[1,128,128]{1,2,0:T(8,128)S(1)} custom-call(f32[1,128,128]{2,1,0:T(8,128)S(1)} %fusion.28), custom_call_target="InvertDiagBlocksLowerTriangular" | custom-call | tf_op jit(solution)/shard_map/jit(_solve_triangular)/triangular_solve | solution.py:82
  98.4 11.7 %cholesky.145 = f32[128,128]{1,0:T(8,128)S(1)} custom-call(f32[128,128]{1,0:T(8,128)S(1)} %fusion.60), custom_call_target="Cholesky" | custom-call | tf_op jit(solution)/shard_map/jit(cholesky)/cholesky | solution.py:81
  111.4 10.0 %custom-call.20 = f32[1,128,128]{1,2,0:T(8,128)S(1)} custom-call(f32[1,128,128]{2,1,0:T(8,128)S(1)} %fusion.29), custom_call_target="InvertDiagBlocksLowerTriangular" | custom-call | tf_op jit(solution)/shard_map/jit(_solve_triangular)/triangular_solve | solution.py:83
  146.9 8.4 %all-to-all-done.1 = bf16[16,32,256]{2,1,0:T(8,128)(2,1)S(1)} async-done(((bf16[16,32,256]{2,1,0:T(8,128)(2,1)}), bf16[16,32,256]{2,1,0:T(8,128)(2,1)S(1)}, u32[]{:S(2)}, u32[]{:S(2)}) %all-to-all-start.1) | async-done | bytes 262176 | tf_op jit(solution)/shard_map/all_to_all | solution.py:15
  155.4 16.1 %all_gather.13 = f32[512,256]{1,0:T(8,128)S(1)} all-gather(f32[32,256]{1,0:T(8,128)S(1)} %convert_reduce_fusion.3), channel_id=1, replica_groups=mesh['tm'=16,'space'=16] {'space'}, dimensions={0}, use_global_device_ids=true | all-gather | bytes 557056 | tf_op jit(solution)/shard_map/all_gather | solution.py:18
  172.7 11.7 %cholesky.156 = f32[128,128]{1,0:T(8,128)S(1)} custom-call(f32[128,128]{1,0:T(8,128)S(1)} %get-tuple-element.17), custom_call_target="Cholesky" | custom-call | tf_op jit(solution)/shard_map/jit(cholesky)/cholesky | solution.py:77
  185.7 9.8 %custom-call.21 = f32[1,128,128]{1,2,0:T(8,128)S(1)} custom-call(f32[1,128,128]{2,1,0:T(8,128)S(1)} %fusion.30), custom_call_target="InvertDiagBlocksLowerTriangular" | custom-call | tf_op jit(solution)/shard_map/jit(_solve_triangular)/triangular_solve | solution.py:82
  196.3 11.7 %cholesky.167 = f32[128,128]{1,0:T(8,128)S(1)} custom-call(f32[128,128]{1,0:T(8,128)S(1)} %fusion.54), custom_call_target="Cholesky" | custom-call | tf_op jit(solution)/shard_map/jit(cholesky)/cholesky | solution.py:81
  209.4 10.2 %custom-call.23 = f32[1,128,128]{1,2,0:T(8,128)S(1)} custom-call(f32[1,128,128]{2,1,0:T(8,128)S(1)} %fusion.31), custom_call_target="InvertDiagBlocksLowerTriangular" | custom-call | tf_op jit(solution)/shard_map/jit(_solve_triangular)/triangular_solve | solution.py:83
  252.1 16.1 %all_gather.14 = f32[512,256]{1,0:T(8,128)S(1)} all-gather(f32[32,256]{1,0:T(8,128)S(1)} %convert_reduce_fusion.2), channel_id=1, replica_groups=mesh['tm'=16,'space'=16] {'space'}, dimensions={0}, use_global_device_ids=true | all-gather | bytes 557056 | tf_op jit(solution)/shard_map/all_gather | solution.py:18
  269.3 11.7 %cholesky.178 = f32[128,128]{1,0:T(8,128)S(1)} custom-call(f32[128,128]{1,0:T(8,128)S(1)} %get-tuple-element.15), custom_call_target="Cholesky" | custom-call | tf_op jit(solution)/shard_map/jit(cholesky)/cholesky | solution.py:77
  282.4 9.8 %custom-call.24 = f32[1,128,128]{1,2,0:T(8,128)S(1)} custom-call(f32[1,128,128]{2,1,0:T(8,128)S(1)} %fusion.32), custom_call_target="InvertDiagBlocksLowerTriangular" | custom-call | tf_op jit(solution)/shard_map/jit(_solve_triangular)/triangular_solve | solution.py:82
  293.0 11.7 %cholesky.189 = f32[128,128]{1,0:T(8,128)S(1)} custom-call(f32[128,128]{1,0:T(8,128)S(1)} %fusion.48), custom_call_target="Cholesky" | custom-call | tf_op jit(solution)/shard_map/jit(cholesky)/cholesky | solution.py:81
  306.0 10.0 %custom-call.26 = f32[1,128,128]{1,2,0:T(8,128)S(1)} custom-call(f32[1,128,128]{2,1,0:T(8,128)S(1)} %fusion.33), custom_call_target="InvertDiagBlocksLowerTriangular" | custom-call | tf_op jit(solution)/shard_map/jit(_solve_triangular)/triangular_solve | solution.py:83
  338.4 11.6 %all-to-all-done.3 = bf16[16,32,256]{2,1,0:T(8,128)(2,1)S(1)} async-done(((bf16[16,32,256]{2,1,0:T(8,128)(2,1)}), bf16[16,32,256]{2,1,0:T(8,128)(2,1)S(1)}, u32[]{:S(2)}, u32[]{:S(2)}) %all-to-all-start.3) | async-done | bytes 262176 | tf_op jit(solution)/shard_map/all_to_all | solution.py:15
  350.1 16.2 %all_gather.15 = f32[512,256]{1,0:T(8,128)S(1)} all-gather(f32[32,256]{1,0:T(8,128)S(1)} %convert_reduce_fusion.1), channel_id=1, replica_groups=mesh['tm'=16,'space'=16] {'space'}, dimensions={0}, use_global_device_ids=true | all-gather | bytes 557056 | tf_op jit(solution)/shard_map/all_gather | solution.py:18
  367.4 11.7 %cholesky.200 = f32[128,128]{1,0:T(8,128)S(1)} custom-call(f32[128,128]{1,0:T(8,128)S(1)} %get-tuple-element.13), custom_call_target="Cholesky" | custom-call | tf_op jit(solution)/shard_map/jit(cholesky)/cholesky | solution.py:77
  380.4 9.8 %custom-call.27 = f32[1,128,128]{1,2,0:T(8,128)S(1)} custom-call(f32[1,128,128]{2,1,0:T(8,128)S(1)} %fusion.34), custom_call_target="InvertDiagBlocksLowerTriangular" | custom-call | tf_op jit(solution)/shard_map/jit(_solve_triangular)/triangular_solve | solution.py:82
  391.5 11.7 %cholesky.211 = f32[128,128]{1,0:T(8,128)S(1)} custom-call(f32[128,128]{1,0:T(8,128)S(1)} %fusion.42), custom_call_target="Cholesky" | custom-call | tf_op jit(solution)/shard_map/jit(cholesky)/cholesky | solution.py:81
  404.5 10.1 %custom-call.29 = f32[1,128,128]{1,2,0:T(8,128)S(1)} custom-call(f32[1,128,128]{2,1,0:T(8,128)S(1)} %fusion.35), custom_call_target="InvertDiagBlocksLowerTriangular" | custom-call | tf_op jit(solution)/shard_map/jit(_solve_triangular)/triangular_solve | solution.py:83
  (157 shorter events, 136.8 us)
Async XLA Ops:
  2.1 16.0 %copy-start.3 = (s32[8,128]{1,0:T(8,128)S(1)}, s32[8,128]{1,0:T(8,128)}, u32[]{:S(2)}) copy-start(s32[8,128]{1,0:T(8,128)} %param.12) | copy-start | bytes 12292
  2.1 16.0 %copy-start.4 = (f32[8,128]{1,0:T(8,128)S(1)}, f32[8,128]{1,0:T(8,128)}, u32[]{:S(2)}) copy-start(f32[8,128]{1,0:T(8,128)} %param.11) | copy-start | bytes 12292
  6.1 6.9 %collective-permute-start = (bf16[256,1,128]{0,2,1:T(8,128)(2,1)S(1)}, bf16[256,1,128]{0,2,1:T(8,128)(2,1)S(1)}, u32[]{:S(2)}, u32[]{:S(2)}) collective-permute-start(bf16[256,1,128]{0,2,1:T(8,128)(2,1)S(1)} %get-tuple-element.10), channel_id=1, source_target_pairs={{0,1},{1,2},{2,3},{3,4},{4,5},{5,6},{6,7},{7,8},{8,9},{9,10},{10,1... | collective-permute-start | bytes 196616 | tf_op jit(solution)/shard_map/ppermute | solution.py:29
  11.0 5.6 %collective-permute-start.1 = (bf16[256,1,128]{0,2,1:T(8,128)(2,1)S(1)}, bf16[256,1,128]{0,2,1:T(8,128)(2,1)S(1)}, u32[]{:S(2)}, u32[]{:S(2)}) collective-permute-start(bf16[256,1,128]{0,2,1:T(8,128)(2,1)S(1)} %get-tuple-element.11), channel_id=1, source_target_pairs={{1,0},{2,1},{3,2},{4,3},{5,4},{6,5},{7,6},{8,7},{9,8},{10,9},{11,1... | collective-permute-start | bytes 196616 | tf_op jit(solution)/shard_map/ppermute | solution.py:31
  16.7 14.6 %collective-permute-start.2 = (bf16[256,10,128]{0,2,1:T(8,128)(2,1)S(1)}, bf16[256,10,128]{0,2,1:T(8,128)(2,1)S(1)}, u32[]{:S(2)}, u32[]{:S(2)}) collective-permute-start(bf16[256,10,128]{0,2,1:T(8,128)(2,1)S(1)} %get-tuple-element.8), channel_id=1, source_target_pairs={{0,16},{16,0},{32,48},{48,32},{64,80},{80,64},{96,112},{112,96},{1... | collective-permute-start | bytes 1966088 | tf_op jit(solution)/shard_map/ppermute | solution.py:39
  32.6 12.8 %copy-start = (bf16[256,3,8,128]{0,3,2,1:T(8,128)(2,1)}, bf16[256,3,8,128]{0,3,2,1:T(8,128)(2,1)S(1)}, u32[]{:S(2)}) copy-start(bf16[256,3,8,128]{0,3,2,1:T(8,128)(2,1)S(1)} %get-tuple-element.25) | copy-start | bytes 4718596
  35.2 21.8 %all-to-all-start = ((bf16[16,32,256]{2,1,0:T(8,128)(2,1)}), bf16[16,32,256]{2,1,0:T(8,128)(2,1)S(1)}, u32[]{:S(2)}, u32[]{:S(2)}) async-start(bf16[16,32,256]{2,1,0:T(8,128)(2,1)} %bitcast.13), calls=%async_computation | async-start | bytes 524288 | tf_op jit(solution)/shard_map/all_to_all | solution.py:15
  47.4 84.8 %collective-permute-start.4 = (bf16[512,3072]{0,1:T(8,128)(2,1)}, bf16[512,3072]{0,1:T(8,128)(2,1)}, u32[]{:S(2)}, u32[]{:S(2)}) collective-permute-start(bf16[512,3072]{0,1:T(8,128)(2,1)} %pad_maximum_fusion), channel_id=1, source_target_pairs={{0,32},{16,48},{32,0},{48,16},{64,96},{80,112},{96,64},{112,80},{1... | collective-permute-start | bytes 9437192 | tf_op jit(solution)/shard_map/ppermute | solution.py:39
  122.9 9.3 %collective-permute-start.3 = (bf16[256,512]{1,0:T(8,128)(2,1)S(1)}, bf16[256,512]{1,0:T(8,128)(2,1)S(1)}, u32[]{:S(2)}, u32[]{:S(2)}) collective-permute-start(bf16[256,512]{1,0:T(8,128)(2,1)S(1)} %fusion.20), channel_id=1, source_target_pairs={{0,32},{16,48},{32,0},{48,16},{64,96},{80,112},{96,64},{112,80},{1... | collective-permute-start | bytes 786440 | tf_op jit(solution)/shard_map/ppermute | solution.py:39
  128.1 15.6 %copy-start.1 = (bf16[256,3072]{1,0:T(8,128)(2,1)}, bf16[256,3072]{1,0:T(8,128)(2,1)S(1)}, u32[]{:S(2)}) copy-start(bf16[256,3072]{1,0:T(8,128)(2,1)S(1)} %convolution_convert_fusion.5) | copy-start | bytes 4718596
  137.7 17.6 %all-to-all-start.1 = ((bf16[16,32,256]{2,1,0:T(8,128)(2,1)}), bf16[16,32,256]{2,1,0:T(8,128)(2,1)S(1)}, u32[]{:S(2)}, u32[]{:S(2)}) async-start(bf16[16,32,256]{2,1,0:T(8,128)(2,1)} %bitcast.25), calls=%async_computation.1 | async-start | bytes 524288 | tf_op jit(solution)/shard_map/all_to_all | solution.py:15
  145.6 83.2 %collective-permute-start.6 = (bf16[512,3072]{1,0:T(8,128)(2,1)}, bf16[512,3072]{1,0:T(8,128)(2,1)}, u32[]{:S(2)}, u32[]{:S(2)}) collective-permute-start(bf16[512,3072]{1,0:T(8,128)(2,1)} %pad_maximum_fusion.1), channel_id=1, source_target_pairs={{0,64},{16,80},{32,96},{48,112},{64,0},{80,16},{96,32},{112,48},{1... | collective-permute-start | bytes 9437192 | tf_op jit(solution)/shard_map/ppermute | solution.py:39
  221.1 7.8 %collective-permute-start.5 = (bf16[256,512]{1,0:T(8,128)(2,1)S(1)}, bf16[256,512]{1,0:T(8,128)(2,1)S(1)}, u32[]{:S(2)}, u32[]{:S(2)}) collective-permute-start(bf16[256,512]{1,0:T(8,128)(2,1)S(1)} %fusion.21), channel_id=1, source_target_pairs={{0,64},{16,80},{32,96},{48,112},{64,0},{80,16},{96,32},{112,48},{1... | collective-permute-start | bytes 786440 | tf_op jit(solution)/shard_map/ppermute | solution.py:39
  224.9 15.6 %copy-start.2 = (bf16[256,3072]{1,0:T(8,128)(2,1)}, bf16[256,3072]{1,0:T(8,128)(2,1)S(1)}, u32[]{:S(2)}) copy-start(bf16[256,3072]{1,0:T(8,128)(2,1)S(1)} %convolution_convert_fusion.3) | copy-start | bytes 4718596
  234.4 17.7 %all-to-all-start.2 = ((bf16[16,32,256]{2,1,0:T(8,128)(2,1)}), bf16[16,32,256]{2,1,0:T(8,128)(2,1)S(1)}, u32[]{:S(2)}, u32[]{:S(2)}) async-start(bf16[16,32,256]{2,1,0:T(8,128)(2,1)} %bitcast.37), calls=%async_computation.2 | async-start | bytes 524288 | tf_op jit(solution)/shard_map/all_to_all | solution.py:15
  242.3 84.5 %collective-permute-start.8 = (bf16[512,3072]{1,0:T(8,128)(2,1)}, bf16[512,3072]{1,0:T(8,128)(2,1)}, u32[]{:S(2)}, u32[]{:S(2)}) collective-permute-start(bf16[512,3072]{1,0:T(8,128)(2,1)} %pad_maximum_fusion.2), channel_id=1, source_target_pairs={{0,128},{16,144},{32,160},{48,176},{64,192},{80,208},{96,224},{112... | collective-permute-start | bytes 9437192 | tf_op jit(solution)/shard_map/ppermute | solution.py:39
  317.5 9.3 %collective-permute-start.7 = (bf16[256,512]{1,0:T(8,128)(2,1)S(1)}, bf16[256,512]{1,0:T(8,128)(2,1)S(1)}, u32[]{:S(2)}, u32[]{:S(2)}) collective-permute-start(bf16[256,512]{1,0:T(8,128)(2,1)S(1)} %fusion.22), channel_id=1, source_target_pairs={{0,128},{16,144},{32,160},{48,176},{64,192},{80,208},{96,224},{112... | collective-permute-start | bytes 786440 | tf_op jit(solution)/shard_map/ppermute | solution.py:39
  322.9 8.7 %copy-start.5 = (bf16[256,3072]{1,0:T(8,128)(2,1)}, bf16[256,3072]{1,0:T(8,128)(2,1)S(1)}, u32[]{:S(2)}) copy-start(bf16[256,3072]{1,0:T(8,128)(2,1)S(1)} %convolution_convert_fusion.1) | copy-start | bytes 4718596
  332.4 17.6 %all-to-all-start.3 = ((bf16[16,32,256]{2,1,0:T(8,128)(2,1)}), bf16[16,32,256]{2,1,0:T(8,128)(2,1)S(1)}, u32[]{:S(2)}, u32[]{:S(2)}) async-start(bf16[16,32,256]{2,1,0:T(8,128)(2,1)} %bitcast.49), calls=%async_computation.3 | async-start | bytes 524288 | tf_op jit(solution)/shard_map/all_to_all | solution.py:15
where the time goes:
time: 424 us; the launch traced here: 419 us
  other arithmetic  198 us (47%)
  blocking collectives  64.8 us (15%)
  waiting for transfers between devices  61.7 us (15%)
  starting transfers between devices  50.7 us (12%)
  matrix products  38.1 us (9%)
    all_gather x4, blocking collectives, summed_rows(): return lax.all_gather(own_rows, axis, axis=0, tiled=True)  64.8 us
    another operation x12, other arithmetic, rotation_of(): jnp.linalg.cholesky(normal[half:, half:] - highest_dot(low_21, low_21.T))  49.6 us
    another operation x12, other arithmetic, rotation_of(): low_11 = jnp.linalg.cholesky(normal[:half, :half])  49.6 us
    another operation x8, other arithmetic, rotation_of(): jax.scipy.linalg.solve_triangular(low_22, mixed_cols[:, half:].T - highes...  42.8 us
    another operation x8, other arithmetic, rotation_of(): jax.scipy.linalg.solve_triangular(low_11, mixed_cols[:, :half].T, lower=T...  41.9 us
    all_to_all x4, waiting for transfers between devices, summed_rows(): parts = lax.all_to_all(shard, axis, 0, 0, tiled=True)  33.7 us
    all_to_all x4, starting transfers between devices, summed_rows(): parts = lax.all_to_all(shard, axis, 0, 0, tiled=True)  28.4 us
    ppermute x7, waiting for transfers between devices, from_partner(): lax.ppermute(shard, axis, [(i, i ^ 1 << stride) for i in range(lax.axis_s...  24.4 us
  transfers between devices with their start and end apart: 13, of which 9 were waited for; matrix products, arithmetic and copies ran while one was open for 39% of the time, Pallas kernels for 0%

commit v1 on v0

--- a/solution.py
+++ b/solution.py
@@ -101,10 +101,16 @@
     mean_state = jnp.mean(stored[0].astype(jnp.float32), axis=0)
     picked = jnp.take(stored[0], snapshot[0], axis=0)
     anomaly = ((picked.astype(jnp.float32) - mean_state) * sea_float).astype(jnp.bfloat16)
+    other_anomaly = from_partner(anomaly, "tm", 0)
     padded = with_halo(anomaly, (("space", 1),), 1)
     basis_now = balance(padded, balance_coef, sea_float)
     levels = lax.axis_size("tm").bit_length() - 1
-    other_padded = from_partner(padded, "tm", 0)
+    other_rims = from_partner(
+        jnp.concatenate([padded[:, :1], padded[:, -1:]], axis=1), "tm", 0
+    )
+    other_padded = jnp.concatenate(
+        [other_rims[:, :1], other_anomaly, other_rims[:, 1:]], axis=1
+    )
     partner = balance(other_padded, balance_coef, sea_float)
     stacked = stack_pair(basis_now, partner)
     for level_idx in range(levels):

time: 424 us -> 416 us (0.981)
  waiting for transfers between devices: 61.7 us -> 52.9 us
    ppermute x7 -> x8, waiting for transfers between devices: 24.4 us -> 16.1 us  [from_partner(): lax.ppermute(shard, axis, [(i, i ^ 1 << stride) for i in range(lax.axis_s...]
    ppermute x7 -> x8, starting transfers between devices: 15.5 us -> 16.6 us  [from_partner(): lax.ppermute(shard, axis, [(i, i ^ 1 << stride) for i in range(lax.axis_s...]
  transfers between devices with their start and end apart: 13 -> 14, of which waited for: 9 -> 9; matrix products, arithmetic and copies ran while one was open for 39% -> 40% of each run, Pallas kernels for 0% -> 0%
where the time goes in v1:
time: 416 us; the launch traced here: 410 us
  other arithmetic  198 us (48%)
  blocking collectives  64.8 us (16%)
  waiting for transfers between devices  52.9 us (13%)
  starting transfers between devices  50.5 us (12%)
  matrix products  38.1 us (9%)
    all_gather x4, blocking collectives, summed_rows(): return lax.all_gather(own_rows, axis, axis=0, tiled=True)  64.8 us
    another operation x12, other arithmetic, rotation_of(): jnp.linalg.cholesky(normal[half:, half:] - highest_dot(low_21, low_21.T))  49.6 us
    another operation x12, other arithmetic, rotation_of(): low_11 = jnp.linalg.cholesky(normal[:half, :half])  49.6 us
    another operation x8, other arithmetic, rotation_of(): jax.scipy.linalg.solve_triangular(low_22, mixed_cols[:, half:].T - highes...  42.8 us
    another operation x8, other arithmetic, rotation_of(): jax.scipy.linalg.solve_triangular(low_11, mixed_cols[:, :half].T, lower=T...  41.9 us
    all_to_all x4, waiting for transfers between devices, summed_rows(): parts = lax.all_to_all(shard, axis, 0, 0, tiled=True)  33.7 us
    all_to_all x4, starting transfers between devices, summed_rows(): parts = lax.all_to_all(shard, axis, 0, 0, tiled=True)  27.6 us
    dot_general x7, matrix products, rotated(): jnp.dot(rotation, stacked, preferred_element_type=jnp.float32)  17.9 us
  transfers between devices with their start and end apart: 14, of which 9 were waited for; matrix products, arithmetic and copies ran while one was open for 40% of the time, Pallas kernels for 0%

profile of v1, /device:TPU:1, one launch (start us, length us, event | category | flops | bytes accessed | tf_op | source)
XLA Modules:
  0.0 409.7 jit_solution(9760586611007248839)
XLA Ops:
  27.1 9.4 %all-to-all-start = ((bf16[16,32,256]{2,1,0:T(8,128)(2,1)}), bf16[16,32,256]{2,1,0:T(8,128)(2,1)S(1)}, u32[]{:S(2)}, u32[]{:S(2)}) async-start(bf16[16,32,256]{2,1,0:T(8,128)(2,1)} %bitcast.13), calls=%async_computation | async-start | bytes 524288 | tf_op jit(solution)/shard_map/all_to_all | solution.py:15
  41.2 6.9 %all-to-all-done = bf16[16,32,256]{2,1,0:T(8,128)(2,1)S(1)} async-done(((bf16[16,32,256]{2,1,0:T(8,128)(2,1)}), bf16[16,32,256]{2,1,0:T(8,128)(2,1)S(1)}, u32[]{:S(2)}, u32[]{:S(2)}) %all-to-all-start) | async-done | bytes 262176 | tf_op jit(solution)/shard_map/all_to_all | solution.py:15
  48.1 16.4 %all_gather.12 = f32[512,256]{1,0:T(8,128)S(1)} all-gather(f32[32,256]{1,0:T(8,128)S(1)} %convert_reduce_fusion.4), channel_id=1, replica_groups=mesh['tm'=16,'space'=16] {'space'}, dimensions={0}, use_global_device_ids=true | all-gather | bytes 557056 | tf_op jit(solution)/shard_map/all_gather | solution.py:18
  65.7 11.7 %cholesky.134 = f32[128,128]{1,0:T(8,128)S(1)} custom-call(f32[128,128]{1,0:T(8,128)S(1)} %get-tuple-element.17), custom_call_target="Cholesky" | custom-call | tf_op jit(solution)/shard_map/jit(cholesky)/cholesky | solution.py:77
  78.8 9.8 %custom-call.18 = f32[1,128,128]{1,2,0:T(8,128)S(1)} custom-call(f32[1,128,128]{2,1,0:T(8,128)S(1)} %fusion.27), custom_call_target="InvertDiagBlocksLowerTriangular" | custom-call | tf_op jit(solution)/shard_map/jit(_solve_triangular)/triangular_solve | solution.py:82
  89.4 11.7 %cholesky.145 = f32[128,128]{1,0:T(8,128)S(1)} custom-call(f32[128,128]{1,0:T(8,128)S(1)} %fusion.59), custom_call_target="Cholesky" | custom-call | tf_op jit(solution)/shard_map/jit(cholesky)/cholesky | solution.py:81
  102.5 10.0 %custom-call.20 = f32[1,128,128]{1,2,0:T(8,128)S(1)} custom-call(f32[1,128,128]{2,1,0:T(8,128)S(1)} %fusion.28), custom_call_target="InvertDiagBlocksLowerTriangular" | custom-call | tf_op jit(solution)/shard_map/jit(_solve_triangular)/triangular_solve | solution.py:83
  137.9 8.4 %all-to-all-done.1 = bf16[16,32,256]{2,1,0:T(8,128)(2,1)S(1)} async-done(((bf16[16,32,256]{2,1,0:T(8,128)(2,1)}), bf16[16,32,256]{2,1,0:T(8,128)(2,1)S(1)}, u32[]{:S(2)}, u32[]{:S(2)}) %all-to-all-start.1) | async-done | bytes 262176 | tf_op jit(solution)/shard_map/all_to_all | solution.py:15
  146.4 16.1 %all_gather.13 = f32[512,256]{1,0:T(8,128)S(1)} all-gather(f32[32,256]{1,0:T(8,128)S(1)} %convert_reduce_fusion.3), channel_id=1, replica_groups=mesh['tm'=16,'space'=16] {'space'}, dimensions={0}, use_global_device_ids=true | all-gather | bytes 557056 | tf_op jit(solution)/shard_map/all_gather | solution.py:18
  163.7 11.7 %cholesky.156 = f32[128,128]{1,0:T(8,128)S(1)} custom-call(f32[128,128]{1,0:T(8,128)S(1)} %get-tuple-element.15), custom_call_target="Cholesky" | custom-call | tf_op jit(solution)/shard_map/jit(cholesky)/cholesky | solution.py:77
  176.7 9.8 %custom-call.21 = f32[1,128,128]{1,2,0:T(8,128)S(1)} custom-call(f32[1,128,128]{2,1,0:T(8,128)S(1)} %fusion.29), custom_call_target="InvertDiagBlocksLowerTriangular" | custom-call | tf_op jit(solution)/shard_map/jit(_solve_triangular)/triangular_solve | solution.py:82
  187.4 11.7 %cholesky.167 = f32[128,128]{1,0:T(8,128)S(1)} custom-call(f32[128,128]{1,0:T(8,128)S(1)} %fusion.53), custom_call_target="Cholesky" | custom-call | tf_op jit(solution)/shard_map/jit(cholesky)/cholesky | solution.py:81
  200.4 10.2 %custom-call.23 = f32[1,128,128]{1,2,0:T(8,128)S(1)} custom-call(f32[1,128,128]{2,1,0:T(8,128)S(1)} %fusion.30), custom_call_target="InvertDiagBlocksLowerTriangular" | custom-call | tf_op jit(solution)/shard_map/jit(_solve_triangular)/triangular_solve | solution.py:83
  243.1 16.1 %all_gather.14 = f32[512,256]{1,0:T(8,128)S(1)} all-gather(f32[32,256]{1,0:T(8,128)S(1)} %convert_reduce_fusion.2), channel_id=1, replica_groups=mesh['tm'=16,'space'=16] {'space'}, dimensions={0}, use_global_device_ids=true | all-gather | bytes 557056 | tf_op jit(solution)/shard_map/all_gather | solution.py:18
  260.4 11.7 %cholesky.178 = f32[128,128]{1,0:T(8,128)S(1)} custom-call(f32[128,128]{1,0:T(8,128)S(1)} %get-tuple-element.13), custom_call_target="Cholesky" | custom-call | tf_op jit(solution)/shard_map/jit(cholesky)/cholesky | solution.py:77
  273.4 9.8 %custom-call.24 = f32[1,128,128]{1,2,0:T(8,128)S(1)} custom-call(f32[1,128,128]{2,1,0:T(8,128)S(1)} %fusion.31), custom_call_target="InvertDiagBlocksLowerTriangular" | custom-call | tf_op jit(solution)/shard_map/jit(_solve_triangular)/triangular_solve | solution.py:82
  284.0 11.7 %cholesky.189 = f32[128,128]{1,0:T(8,128)S(1)} custom-call(f32[128,128]{1,0:T(8,128)S(1)} %fusion.47), custom_call_target="Cholesky" | custom-call | tf_op jit(solution)/shard_map/jit(cholesky)/cholesky | solution.py:81
  297.1 10.0 %custom-call.26 = f32[1,128,128]{1,2,0:T(8,128)S(1)} custom-call(f32[1,128,128]{2,1,0:T(8,128)S(1)} %fusion.32), custom_call_target="InvertDiagBlocksLowerTriangular" | custom-call | tf_op jit(solution)/shard_map/jit(_solve_triangular)/triangular_solve | solution.py:83
  329.5 11.6 %all-to-all-done.3 = bf16[16,32,256]{2,1,0:T(8,128)(2,1)S(1)} async-done(((bf16[16,32,256]{2,1,0:T(8,128)(2,1)}), bf16[16,32,256]{2,1,0:T(8,128)(2,1)S(1)}, u32[]{:S(2)}, u32[]{:S(2)}) %all-to-all-start.3) | async-done | bytes 262176 | tf_op jit(solution)/shard_map/all_to_all | solution.py:15
  341.1 16.2 %all_gather.15 = f32[512,256]{1,0:T(8,128)S(1)} all-gather(f32[32,256]{1,0:T(8,128)S(1)} %convert_reduce_fusion.1), channel_id=1, replica_groups=mesh['tm'=16,'space'=16] {'space'}, dimensions={0}, use_global_device_ids=true | all-gather | bytes 557056 | tf_op jit(solution)/shard_map/all_gather | solution.py:18
  358.4 11.7 %cholesky.200 = f32[128,128]{1,0:T(8,128)S(1)} custom-call(f32[128,128]{1,0:T(8,128)S(1)} %get-tuple-element.11), custom_call_target="Cholesky" | custom-call | tf_op jit(solution)/shard_map/jit(cholesky)/cholesky | solution.py:77
  371.5 9.8 %custom-call.27 = f32[1,128,128]{1,2,0:T(8,128)S(1)} custom-call(f32[1,128,128]{2,1,0:T(8,128)S(1)} %fusion.33), custom_call_target="InvertDiagBlocksLowerTriangular" | custom-call | tf_op jit(solution)/shard_map/jit(_solve_triangular)/triangular_solve | solution.py:82
  382.5 11.7 %cholesky.211 = f32[128,128]{1,0:T(8,128)S(1)} custom-call(f32[128,128]{1,0:T(8,128)S(1)} %fusion.41), custom_call_target="Cholesky" | custom-call | tf_op jit(solution)/shard_map/jit(cholesky)/cholesky | solution.py:81
  395.6 10.1 %custom-call.29 = f32[1,128,128]{1,2,0:T(8,128)S(1)} custom-call(f32[1,128,128]{2,1,0:T(8,128)S(1)} %fusion.34), custom_call_target="InvertDiagBlocksLowerTriangular" | custom-call | tf_op jit(solution)/shard_map/jit(_solve_triangular)/triangular_solve | solution.py:83
  (160 shorter events, 134.2 us)
Async XLA Ops:
  0.0 14.9 %copy-start.3 = (s32[8,128]{1,0:T(8,128)S(1)}, s32[8,128]{1,0:T(8,128)}, u32[]{:S(2)}) copy-start(s32[8,128]{1,0:T(8,128)} %param.12) | copy-start | bytes 12292
  0.0 14.9 %copy-start.4 = (f32[8,128]{1,0:T(8,128)S(1)}, f32[8,128]{1,0:T(8,128)}, u32[]{:S(2)}) copy-start(f32[8,128]{1,0:T(8,128)} %param.11) | copy-start | bytes 12292
  6.1 17.1 %collective-permute-start.2 = (bf16[256,8,128]{0,2,1:T(8,128)(2,1)S(1)}, bf16[256,8,128]{0,2,1:T(8,128)(2,1)S(1)}, u32[]{:S(2)}, u32[]{:S(2)}) collective-permute-start(bf16[256,8,128]{0,2,1:T(8,128)(2,1)S(1)} %multiply_convert_fusion), channel_id=1, source_target_pairs={{0,16},{16,0},{32,48},{48,32},{64,80},{80,64},{96,112},{112,96},{1... | collective-permute-start | bytes 1572872 | tf_op jit(solution)/shard_map/ppermute | solution.py:39
  8.2 7.2 %collective-permute-start = (bf16[256,1,128]{0,2,1:T(8,128)(2,1)S(1)}, bf16[256,1,128]{0,2,1:T(8,128)(2,1)S(1)}, u32[]{:S(2)}, u32[]{:S(2)}) collective-permute-start(bf16[256,1,128]{0,2,1:T(8,128)(2,1)S(1)} %get-tuple-element.6), channel_id=1, source_target_pairs={{0,1},{1,2},{2,3},{3,4},{4,5},{5,6},{6,7},{7,8},{8,9},{9,10},{10,1... | collective-permute-start | bytes 196616 | tf_op jit(solution)/shard_map/ppermute | solution.py:29
  12.6 5.9 %collective-permute-start.1 = (bf16[256,1,128]{0,2,1:T(8,128)(2,1)S(1)}, bf16[256,1,128]{0,2,1:T(8,128)(2,1)S(1)}, u32[]{:S(2)}, u32[]{:S(2)}) collective-permute-start(bf16[256,1,128]{0,2,1:T(8,128)(2,1)S(1)} %get-tuple-element.8), channel_id=1, source_target_pairs={{1,0},{2,1},{3,2},{4,3},{5,4},{6,5},{7,6},{8,7},{9,8},{10,9},{11,1... | collective-permute-start | bytes 196616 | tf_op jit(solution)/shard_map/ppermute | solution.py:31
  18.5 4.7 %collective-permute-start.3 = (bf16[256,2,128]{0,2,1:T(8,128)(2,1)S(1)}, bf16[256,2,128]{0,2,1:T(8,128)(2,1)S(1)}, u32[]{:S(2)}, u32[]{:S(2)}) collective-permute-start(bf16[256,2,128]{0,2,1:T(8,128)(2,1)S(1)} %pad_maximum_fusion.10), channel_id=1, source_target_pairs={{0,16},{16,0},{32,48},{48,32},{64,80},{80,64},{96,112},{112,96},{1... | collective-permute-start | bytes 393224 | tf_op jit(solution)/shard_map/ppermute | solution.py:39
  24.5 12.0 %copy-start = (bf16[256,3,8,128]{0,3,2,1:T(8,128)(2,1)}, bf16[256,3,8,128]{0,3,2,1:T(8,128)(2,1)S(1)}, u32[]{:S(2)}) copy-start(bf16[256,3,8,128]{0,3,2,1:T(8,128)(2,1)S(1)} %get-tuple-element.25) | copy-start | bytes 4718596
  27.1 21.0 %all-to-all-start = ((bf16[16,32,256]{2,1,0:T(8,128)(2,1)}), bf16[16,32,256]{2,1,0:T(8,128)(2,1)S(1)}, u32[]{:S(2)}, u32[]{:S(2)}) async-start(bf16[16,32,256]{2,1,0:T(8,128)(2,1)} %bitcast.13), calls=%async_computation | async-start | bytes 524288 | tf_op jit(solution)/shard_map/all_to_all | solution.py:15
  38.4 84.8 %collective-permute-start.5 = (bf16[512,3072]{0,1:T(8,128)(2,1)}, bf16[512,3072]{0,1:T(8,128)(2,1)}, u32[]{:S(2)}, u32[]{:S(2)}) collective-permute-start(bf16[512,3072]{0,1:T(8,128)(2,1)} %pad_maximum_fusion), channel_id=1, source_target_pairs={{0,32},{16,48},{32,0},{48,16},{64,96},{80,112},{96,64},{112,80},{1... | collective-permute-start | bytes 9437192 | tf_op jit(solution)/shard_map/ppermute | solution.py:39
  113.9 9.3 %collective-permute-start.4 = (bf16[256,512]{1,0:T(8,128)(2,1)S(1)}, bf16[256,512]{1,0:T(8,128)(2,1)S(1)}, u32[]{:S(2)}, u32[]{:S(2)}) collective-permute-start(bf16[256,512]{1,0:T(8,128)(2,1)S(1)} %fusion.20), channel_id=1, source_target_pairs={{0,32},{16,48},{32,0},{48,16},{64,96},{80,112},{96,64},{112,80},{1... | collective-permute-start | bytes 786440 | tf_op jit(solution)/shard_map/ppermute | solution.py:39
  119.2 15.6 %copy-start.1 = (bf16[256,3072]{1,0:T(8,128)(2,1)}, bf16[256,3072]{1,0:T(8,128)(2,1)S(1)}, u32[]{:S(2)}) copy-start(bf16[256,3072]{1,0:T(8,128)(2,1)S(1)} %convolution_convert_fusion.5) | copy-start | bytes 4718596
  128.7 17.6 %all-to-all-start.1 = ((bf16[16,32,256]{2,1,0:T(8,128)(2,1)}), bf16[16,32,256]{2,1,0:T(8,128)(2,1)S(1)}, u32[]{:S(2)}, u32[]{:S(2)}) async-start(bf16[16,32,256]{2,1,0:T(8,128)(2,1)} %bitcast.25), calls=%async_computation.1 | async-start | bytes 524288 | tf_op jit(solution)/shard_map/all_to_all | solution.py:15
  136.6 83.2 %collective-permute-start.7 = (bf16[512,3072]{1,0:T(8,128)(2,1)}, bf16[512,3072]{1,0:T(8,128)(2,1)}, u32[]{:S(2)}, u32[]{:S(2)}) collective-permute-start(bf16[512,3072]{1,0:T(8,128)(2,1)} %pad_maximum_fusion.1), channel_id=1, source_target_pairs={{0,64},{16,80},{32,96},{48,112},{64,0},{80,16},{96,32},{112,48},{1... | collective-permute-start | bytes 9437192 | tf_op jit(solution)/shard_map/ppermute | solution.py:39
  212.1 7.8 %collective-permute-start.6 = (bf16[256,512]{1,0:T(8,128)(2,1)S(1)}, bf16[256,512]{1,0:T(8,128)(2,1)S(1)}, u32[]{:S(2)}, u32[]{:S(2)}) collective-permute-start(bf16[256,512]{1,0:T(8,128)(2,1)S(1)} %fusion.21), channel_id=1, source_target_pairs={{0,64},{16,80},{32,96},{48,112},{64,0},{80,16},{96,32},{112,48},{1... | collective-permute-start | bytes 786440 | tf_op jit(solution)/shard_map/ppermute | solution.py:39
  215.9 15.6 %copy-start.2 = (bf16[256,3072]{1,0:T(8,128)(2,1)}, bf16[256,3072]{1,0:T(8,128)(2,1)S(1)}, u32[]{:S(2)}) copy-start(bf16[256,3072]{1,0:T(8,128)(2,1)S(1)} %convolution_convert_fusion.3) | copy-start | bytes 4718596
  225.4 17.7 %all-to-all-start.2 = ((bf16[16,32,256]{2,1,0:T(8,128)(2,1)}), bf16[16,32,256]{2,1,0:T(8,128)(2,1)S(1)}, u32[]{:S(2)}, u32[]{:S(2)}) async-start(bf16[16,32,256]{2,1,0:T(8,128)(2,1)} %bitcast.37), calls=%async_computation.2 | async-start | bytes 524288 | tf_op jit(solution)/shard_map/all_to_all | solution.py:15
  233.4 84.5 %collective-permute-start.9 = (bf16[512,3072]{1,0:T(8,128)(2,1)}, bf16[512,3072]{1,0:T(8,128)(2,1)}, u32[]{:S(2)}, u32[]{:S(2)}) collective-permute-start(bf16[512,3072]{1,0:T(8,128)(2,1)} %pad_maximum_fusion.2), channel_id=1, source_target_pairs={{0,128},{16,144},{32,160},{48,176},{64,192},{80,208},{96,224},{112... | collective-permute-start | bytes 9437192 | tf_op jit(solution)/shard_map/ppermute | solution.py:39
  308.6 9.3 %collective-permute-start.8 = (bf16[256,512]{1,0:T(8,128)(2,1)S(1)}, bf16[256,512]{1,0:T(8,128)(2,1)S(1)}, u32[]{:S(2)}, u32[]{:S(2)}) collective-permute-start(bf16[256,512]{1,0:T(8,128)(2,1)S(1)} %fusion.22), channel_id=1, source_target_pairs={{0,128},{16,144},{32,160},{48,176},{64,192},{80,208},{96,224},{112... | collective-permute-start | bytes 786440 | tf_op jit(solution)/shard_map/ppermute | solution.py:39
  314.0 8.7 %copy-start.5 = (bf16[256,3072]{1,0:T(8,128)(2,1)}, bf16[256,3072]{1,0:T(8,128)(2,1)S(1)}, u32[]{:S(2)}) copy-start(bf16[256,3072]{1,0:T(8,128)(2,1)S(1)} %convolution_convert_fusion.1) | copy-start | bytes 4718596
  323.4 17.7 %all-to-all-start.3 = ((bf16[16,32,256]{2,1,0:T(8,128)(2,1)}), bf16[16,32,256]{2,1,0:T(8,128)(2,1)S(1)}, u32[]{:S(2)}, u32[]{:S(2)}) async-start(bf16[16,32,256]{2,1,0:T(8,128)(2,1)} %bitcast.49), calls=%async_computation.3 | async-start | bytes 524288 | tf_op jit(solution)/shard_map/all_to_all | solution.py:15

commit v2 on v1

--- a/solution.py
+++ b/solution.py
@@ -4,10 +4,6 @@
 from jax.sharding import PartitionSpec as P
 
 inv_root2 = 0.7071067811865476
-
-
-def gathered_total(shard, axis):
-    return lax.all_gather(shard, axis).astype(jnp.float32).sum(0)
 
 
 def summed_rows(shard, axis):
@@ -83,7 +79,9 @@
     lower_rows = jax.scipy.linalg.solve_triangular(
         low_22, mixed_cols[:, half:].T - highest_dot(low_21, upper_rows), lower=True
     )
-    return (jnp.concatenate([upper_rows, lower_rows], axis=0) * inv_root2).astype(jnp.bfloat16)
+    return (upper_rows * inv_root2).astype(jnp.bfloat16), (lower_rows * inv_root2).astype(
+        jnp.bfloat16
+    )
 
 
 def highest_dot(left, right):
@@ -115,7 +113,7 @@
     stacked = stack_pair(basis_now, partner)
     for level_idx in range(levels):
         if level_idx == levels - 1:
-            rotation = rotation_of(stacked)
+            rotation = jnp.concatenate(rotation_of(stacked), axis=0)
             member_share = rotation.shape[0] // lax.axis_size("tm")
             rotation = lax.dynamic_slice_in_dim(
                 rotation, lax.axis_index("tm") * member_share, member_share, 0
@@ -123,10 +121,13 @@
             basis_now = rotated(rotation, stacked)
         else:
             partner_stacked = from_partner(stacked, "tm", level_idx + 1)
-            rotation = rotation_of(stacked)
-            partner_rotation = from_partner(rotation, "tm", level_idx + 1)
-            basis_now = rotated(rotation, stacked)
-            partner = rotated(partner_rotation, partner_stacked)
+            halves = rotation_of(stacked)
+            partner_upper = from_partner(halves[0], "tm", level_idx + 1)
+            partner_halves = [partner_upper, from_partner(halves[1], "tm", level_idx + 1)]
+            basis_now = jnp.concatenate([rotated(half, stacked) for half in halves], axis=0)
+            partner = jnp.concatenate(
+                [rotated(half, partner_stacked) for half in partner_halves], axis=0
+            )
             stacked = stack_pair(basis_now, partner)
     return basis_now.reshape(basis_now.shape[0], 3, stored.shape[2], stored.shape[3])
 
@@ -134,5 +135,6 @@
 def solution(mesh):
     placed = (P("tm", None, "space", None), P("tm", None), P("space", None), P("space", None))
     return jax.shard_map(
-        body, mesh=mesh, in_specs=placed, out_specs=P("tm", None, "space", None), check_vma=False
+        body, mesh=mesh, in_specs=placed, out_specs=P("tm", None, "space", None),
+        check_vma=False,
     )

time: 416 us -> 441 us (1.060)
  matrix products: 38.1 us -> 50.2 us
  other arithmetic: 198 us -> 205 us
    another operation x8, other arithmetic: 41.9 us -> 48 us  [rotation_of(): jax.scipy.linalg.solve_triangular(low_11, mixed_cols[:, :half].T, lower=T...]
    dot_general x7 -> x13, matrix products: 17.9 us -> 21.6 us  [rotated(): jnp.dot(rotation, stacked, preferred_element_type=jnp.float32)]
    ppermute x8 -> x11, waiting for transfers between devices: 16.1 us -> 14.2 us  [from_partner(): lax.ppermute(shard, axis, [(i, i ^ 1 << stride) for i in range(lax.axis_s...]
    ppermute x8 -> x11, starting transfers between devices: 16.6 us -> 17.1 us  [from_partner(): lax.ppermute(shard, axis, [(i, i ^ 1 << stride) for i in range(lax.axis_s...]
  transfers between devices with their start and end apart: 14 -> 17, of which waited for: 9 -> 11; matrix products, arithmetic and copies ran while one was open for 40% -> 42% of each run, Pallas kernels for 0% -> 0%
where the time goes in v2:
time: 441 us; the launch traced here: 434 us
  other arithmetic  205 us (46%)
  blocking collectives  64.6 us (15%)
  waiting for transfers between devices  55 us (12%)
  starting transfers between devices  51.8 us (12%)
  matrix products  50.2 us (11%)
  local copies, waits for them, and re-layouts  6.39 us (1%)
    all_gather x4, blocking collectives, summed_rows(): return lax.all_gather(own_rows, axis, axis=0, tiled=True)  64.6 us
    another operation x12, other arithmetic, rotation_of(): low_11 = jnp.linalg.cholesky(normal[:half, :half])  52.1 us
    another operation x12, other arithmetic, rotation_of(): jnp.linalg.cholesky(normal[half:, half:] - highest_dot(low_21, low_21.T))  49.6 us
    another operation x8, other arithmetic, rotation_of(): jax.scipy.linalg.solve_triangular(low_11, mixed_cols[:, :half].T, lower=T...  48 us
    another operation x8, other arithmetic, rotation_of(): jax.scipy.linalg.solve_triangular(low_22, mixed_cols[:, half:].T - highes...  42.8 us
    all_to_all x4, waiting for transfers between devices, summed_rows(): parts = lax.all_to_all(shard, axis, 0, 0, tiled=True)  37.7 us
    all_to_all x4, starting transfers between devices, summed_rows(): parts = lax.all_to_all(shard, axis, 0, 0, tiled=True)  28.4 us
    dot_general x13, matrix products, rotated(): jnp.dot(rotation, stacked, preferred_element_type=jnp.float32)  21.6 us
  transfers between devices with their start and end apart: 17, of which 11 were waited for; matrix products, arithmetic and copies ran while one was open for 42% of the time, Pallas kernels for 0%

profile of v2, /device:TPU:1, one launch (start us, length us, event | category | flops | bytes accessed | tf_op | source)
XLA Modules:
  0.0 434.5 jit_solution(6961530497376901716)
XLA Ops:
  27.1 9.4 %all-to-all-start = ((bf16[16,32,256]{2,1,0:T(8,128)(2,1)}), bf16[16,32,256]{2,1,0:T(8,128)(2,1)S(1)}, u32[]{:S(2)}, u32[]{:S(2)}) async-start(bf16[16,32,256]{2,1,0:T(8,128)(2,1)} %bitcast.13), calls=%async_computation | async-start | bytes 524288 | tf_op jit(solution)/shard_map/all_to_all | solution.py:11
  48.2 16.1 %all_gather.12 = f32[512,256]{1,0:T(8,128)S(1)} all-gather(f32[32,256]{1,0:T(8,128)S(1)} %convert_reduce_fusion.4), channel_id=1, replica_groups=mesh['tm'=16,'space'=16] {'space'}, dimensions={0}, use_global_device_ids=true | all-gather | bytes 557056 | tf_op jit(solution)/shard_map/all_gather | solution.py:14
  66.8 12.5 %cholesky.134 = f32[128,128]{1,0:T(8,128)S(1)} custom-call(f32[128,128]{1,0:T(8,128)} %get-tuple-element.17), custom_call_target="Cholesky" | custom-call | tf_op jit(solution)/shard_map/jit(cholesky)/cholesky | solution.py:73
  81.5 11.3 %custom-call.18 = f32[1,128,128]{1,2,0:T(8,128)} custom-call(f32[1,128,128]{2,1,0:T(8,128)} %fusion.28), custom_call_target="InvertDiagBlocksLowerTriangular" | custom-call | tf_op jit(solution)/shard_map/jit(_solve_triangular)/triangular_solve | solution.py:78
  94.4 11.7 %cholesky.145 = f32[128,128]{1,0:T(8,128)S(1)} custom-call(f32[128,128]{1,0:T(8,128)S(1)} %fusion.56), custom_call_target="Cholesky" | custom-call | tf_op jit(solution)/shard_map/jit(cholesky)/cholesky | solution.py:77
  107.5 10.0 %custom-call.20 = f32[1,128,128]{1,2,0:T(8,128)S(1)} custom-call(f32[1,128,128]{2,1,0:T(8,128)S(1)} %fusion.29), custom_call_target="InvertDiagBlocksLowerTriangular" | custom-call | tf_op jit(solution)/shard_map/jit(_solve_triangular)/triangular_solve | solution.py:79
  146.0 10.3 %all-to-all-done.1 = bf16[16,32,256]{2,1,0:T(8,128)(2,1)S(1)} async-done(((bf16[16,32,256]{2,1,0:T(8,128)(2,1)}), bf16[16,32,256]{2,1,0:T(8,128)(2,1)S(1)}, u32[]{:S(2)}, u32[]{:S(2)}) %all-to-all-start.1) | async-done | bytes 262176 | tf_op jit(solution)/shard_map/all_to_all | solution.py:11
  156.3 16.3 %all_gather.13 = f32[512,256]{1,0:T(8,128)S(1)} all-gather(f32[32,256]{1,0:T(8,128)S(1)} %convert_reduce_fusion.3), channel_id=1, replica_groups=mesh['tm'=16,'space'=16] {'space'}, dimensions={0}, use_global_device_ids=true | all-gather | bytes 557056 | tf_op jit(solution)/shard_map/all_gather | solution.py:14
  175.2 12.5 %cholesky.156 = f32[128,128]{1,0:T(8,128)S(1)} custom-call(f32[128,128]{1,0:T(8,128)} %get-tuple-element.15), custom_call_target="Cholesky" | custom-call | tf_op jit(solution)/shard_map/jit(cholesky)/cholesky | solution.py:73
  189.6 11.3 %custom-call.21 = f32[1,128,128]{1,2,0:T(8,128)} custom-call(f32[1,128,128]{2,1,0:T(8,128)} %fusion.30), custom_call_target="InvertDiagBlocksLowerTriangular" | custom-call | tf_op jit(solution)/shard_map/jit(_solve_triangular)/triangular_solve | solution.py:78
  202.6 11.7 %cholesky.167 = f32[128,128]{1,0:T(8,128)S(1)} custom-call(f32[128,128]{1,0:T(8,128)S(1)} %fusion.51), custom_call_target="Cholesky" | custom-call | tf_op jit(solution)/shard_map/jit(cholesky)/cholesky | solution.py:77
  215.6 10.0 %custom-call.23 = f32[1,128,128]{1,2,0:T(8,128)S(1)} custom-call(f32[1,128,128]{2,1,0:T(8,128)S(1)} %fusion.31), custom_call_target="InvertDiagBlocksLowerTriangular" | custom-call | tf_op jit(solution)/shard_map/jit(_solve_triangular)/triangular_solve | solution.py:79
  250.6 9.0 %all-to-all-done.2 = bf16[16,32,256]{2,1,0:T(8,128)(2,1)S(1)} async-done(((bf16[16,32,256]{2,1,0:T(8,128)(2,1)}), bf16[16,32,256]{2,1,0:T(8,128)(2,1)S(1)}, u32[]{:S(2)}, u32[]{:S(2)}) %all-to-all-start.2) | async-done | bytes 262176 | tf_op jit(solution)/shard_map/all_to_all | solution.py:11
  259.6 16.1 %all_gather.14 = f32[512,256]{1,0:T(8,128)S(1)} all-gather(f32[32,256]{1,0:T(8,128)S(1)} %convert_reduce_fusion.2), channel_id=1, replica_groups=mesh['tm'=16,'space'=16] {'space'}, dimensions={0}, use_global_device_ids=true | all-gather | bytes 557056 | tf_op jit(solution)/shard_map/all_gather | solution.py:14
  278.4 12.5 %cholesky.178 = f32[128,128]{1,0:T(8,128)S(1)} custom-call(f32[128,128]{1,0:T(8,128)} %get-tuple-element.13), custom_call_target="Cholesky" | custom-call | tf_op jit(solution)/shard_map/jit(cholesky)/cholesky | solution.py:73
  292.8 11.3 %custom-call.24 = f32[1,128,128]{1,2,0:T(8,128)} custom-call(f32[1,128,128]{2,1,0:T(8,128)} %fusion.32), custom_call_target="InvertDiagBlocksLowerTriangular" | custom-call | tf_op jit(solution)/shard_map/jit(_solve_triangular)/triangular_solve | solution.py:78
  305.7 11.7 %cholesky.189 = f32[128,128]{1,0:T(8,128)S(1)} custom-call(f32[128,128]{1,0:T(8,128)S(1)} %fusion.46), custom_call_target="Cholesky" | custom-call | tf_op jit(solution)/shard_map/jit(cholesky)/cholesky | solution.py:77
  318.7 10.2 %custom-call.26 = f32[1,128,128]{1,2,0:T(8,128)S(1)} custom-call(f32[1,128,128]{2,1,0:T(8,128)S(1)} %fusion.33), custom_call_target="InvertDiagBlocksLowerTriangular" | custom-call | tf_op jit(solution)/shard_map/jit(_solve_triangular)/triangular_solve | solution.py:79
  354.0 11.6 %all-to-all-done.3 = bf16[16,32,256]{2,1,0:T(8,128)(2,1)S(1)} async-done(((bf16[16,32,256]{2,1,0:T(8,128)(2,1)}), bf16[16,32,256]{2,1,0:T(8,128)(2,1)S(1)}, u32[]{:S(2)}, u32[]{:S(2)}) %all-to-all-start.3) | async-done | bytes 262176 | tf_op jit(solution)/shard_map/all_to_all | solution.py:11
  365.6 16.1 %all_gather.15 = f32[512,256]{1,0:T(8,128)S(1)} all-gather(f32[32,256]{1,0:T(8,128)S(1)} %convert_reduce_fusion.1), channel_id=1, replica_groups=mesh['tm'=16,'space'=16] {'space'}, dimensions={0}, use_global_device_ids=true | all-gather | bytes 557056 | tf_op jit(solution)/shard_map/all_gather | solution.py:14
  382.9 11.7 %cholesky.200 = f32[128,128]{1,0:T(8,128)S(1)} custom-call(f32[128,128]{1,0:T(8,128)S(1)} %get-tuple-element.11), custom_call_target="Cholesky" | custom-call | tf_op jit(solution)/shard_map/jit(cholesky)/cholesky | solution.py:73
  395.9 9.8 %custom-call.27 = f32[1,128,128]{1,2,0:T(8,128)S(1)} custom-call(f32[1,128,128]{2,1,0:T(8,128)S(1)} %fusion.34), custom_call_target="InvertDiagBlocksLowerTriangular" | custom-call | tf_op jit(solution)/shard_map/jit(_solve_triangular)/triangular_solve | solution.py:78
  407.0 11.7 %cholesky.211 = f32[128,128]{1,0:T(8,128)S(1)} custom-call(f32[128,128]{1,0:T(8,128)S(1)} %fusion.41), custom_call_target="Cholesky" | custom-call | tf_op jit(solution)/shard_map/jit(cholesky)/cholesky | solution.py:77
  420.0 10.0 %custom-call.29 = f32[1,128,128]{1,2,0:T(8,128)S(1)} custom-call(f32[1,128,128]{2,1,0:T(8,128)S(1)} %fusion.35), custom_call_target="InvertDiagBlocksLowerTriangular" | custom-call | tf_op jit(solution)/shard_map/jit(_solve_triangular)/triangular_solve | solution.py:79
  (185 shorter events, 148.6 us)
Async XLA Ops:
  0.0 14.9 %copy-start.12 = (s32[8,128]{1,0:T(8,128)S(1)}, s32[8,128]{1,0:T(8,128)}, u32[]{:S(2)}) copy-start(s32[8,128]{1,0:T(8,128)} %param.12) | copy-start | bytes 12292
  0.0 14.9 %copy-start.13 = (f32[8,128]{1,0:T(8,128)S(1)}, f32[8,128]{1,0:T(8,128)}, u32[]{:S(2)}) copy-start(f32[8,128]{1,0:T(8,128)} %param.11) | copy-start | bytes 12292
  6.1 17.1 %collective-permute-start.2 = (bf16[256,8,128]{0,2,1:T(8,128)(2,1)S(1)}, bf16[256,8,128]{0,2,1:T(8,128)(2,1)S(1)}, u32[]{:S(2)}, u32[]{:S(2)}) collective-permute-start(bf16[256,8,128]{0,2,1:T(8,128)(2,1)S(1)} %multiply_convert_fusion), channel_id=1, source_target_pairs={{0,16},{16,0},{32,48},{48,32},{64,80},{80,64},{96,112},{112,96},{1... | collective-permute-start | bytes 1572872 | tf_op jit(solution)/shard_map/ppermute | solution.py:35
  8.2 7.2 %collective-permute-start = (bf16[256,1,128]{0,2,1:T(8,128)(2,1)S(1)}, bf16[256,1,128]{0,2,1:T(8,128)(2,1)S(1)}, u32[]{:S(2)}, u32[]{:S(2)}) collective-permute-start(bf16[256,1,128]{0,2,1:T(8,128)(2,1)S(1)} %get-tuple-element.6), channel_id=1, source_target_pairs={{0,1},{1,2},{2,3},{3,4},{4,5},{5,6},{6,7},{7,8},{8,9},{9,10},{10,1... | collective-permute-start | bytes 196616 | tf_op jit(solution)/shard_map/ppermute | solution.py:25
  12.6 5.9 %collective-permute-start.1 = (bf16[256,1,128]{0,2,1:T(8,128)(2,1)S(1)}, bf16[256,1,128]{0,2,1:T(8,128)(2,1)S(1)}, u32[]{:S(2)}, u32[]{:S(2)}) collective-permute-start(bf16[256,1,128]{0,2,1:T(8,128)(2,1)S(1)} %get-tuple-element.8), channel_id=1, source_target_pairs={{1,0},{2,1},{3,2},{4,3},{5,4},{6,5},{7,6},{8,7},{9,8},{10,9},{11,1... | collective-permute-start | bytes 196616 | tf_op jit(solution)/shard_map/ppermute | solution.py:27
  18.5 4.7 %collective-permute-start.3 = (bf16[256,2,128]{0,2,1:T(8,128)(2,1)S(1)}, bf16[256,2,128]{0,2,1:T(8,128)(2,1)S(1)}, u32[]{:S(2)}, u32[]{:S(2)}) collective-permute-start(bf16[256,2,128]{0,2,1:T(8,128)(2,1)S(1)} %pad_maximum_fusion.8), channel_id=1, source_target_pairs={{0,16},{16,0},{32,48},{48,32},{64,80},{80,64},{96,112},{112,96},{1... | collective-permute-start | bytes 393224 | tf_op jit(solution)/shard_map/ppermute | solution.py:35
  24.5 12.0 %copy-start.3 = (bf16[256,3,8,128]{0,3,2,1:T(8,128)(2,1)}, bf16[256,3,8,128]{0,3,2,1:T(8,128)(2,1)S(1)}, u32[]{:S(2)}) copy-start(bf16[256,3,8,128]{0,3,2,1:T(8,128)(2,1)S(1)} %get-tuple-element.32) | copy-start | bytes 4718596
  24.5 12.0 %copy-start.5 = (bf16[256,3,8,128]{0,3,2,1:T(8,128)(2,1)}, bf16[256,3,8,128]{0,3,2,1:T(8,128)(2,1)S(1)}, u32[]{:S(2)}) copy-start(bf16[256,3,8,128]{0,3,2,1:T(8,128)(2,1)S(1)} %get-tuple-element.33) | copy-start | bytes 4718596
  27.1 21.0 %all-to-all-start = ((bf16[16,32,256]{2,1,0:T(8,128)(2,1)}), bf16[16,32,256]{2,1,0:T(8,128)(2,1)S(1)}, u32[]{:S(2)}, u32[]{:S(2)}) async-start(bf16[16,32,256]{2,1,0:T(8,128)(2,1)} %bitcast.13), calls=%async_computation | async-start | bytes 524288 | tf_op jit(solution)/shard_map/all_to_all | solution.py:11
  38.5 90.0 %collective-permute-start.5 = (bf16[512,3072]{0,1:T(8,128)(2,1)}, bf16[512,3072]{0,1:T(8,128)(2,1)S(1)}, u32[]{:S(2)}, u32[]{:S(2)}) collective-permute-start(bf16[512,3072]{0,1:T(8,128)(2,1)} %pad_maximum_fusion), channel_id=1, source_target_pairs={{0,32},{16,48},{32,0},{48,16},{64,96},{80,112},{96,64},{112,80},{1... | collective-permute-start | bytes 9437192 | tf_op jit(solution)/shard_map/ppermute | solution.py:35
  118.9 9.6 %collective-permute-start.4 = (bf16[128,512]{1,0:T(8,128)(2,1)S(1)}, bf16[128,512]{1,0:T(8,128)(2,1)S(1)}, u32[]{:S(2)}, u32[]{:S(2)}) collective-permute-start(bf16[128,512]{1,0:T(8,128)(2,1)S(1)} %get-tuple-element.24), channel_id=1, source_target_pairs={{0,32},{16,48},{32,0},{48,16},{64,96},{80,112},{96,64},{112,80},{1... | collective-permute-start | bytes 393224 | tf_op jit(solution)/shard_map/ppermute | solution.py:35
  128.1 6.2 %collective-permute-start.6 = (bf16[128,512]{1,0:T(8,128)(2,1)S(1)}, bf16[128,512]{1,0:T(8,128)(2,1)S(1)}, u32[]{:S(2)}, u32[]{:S(2)}) collective-permute-start(bf16[128,512]{1,0:T(8,128)(2,1)S(1)} %fusion.4), channel_id=1, source_target_pairs={{0,32},{16,48},{32,0},{48,16},{64,96},{80,112},{96,64},{112,80},{1... | collective-permute-start | bytes 393224 | tf_op jit(solution)/shard_map/ppermute | solution.py:35
  138.4 17.9 %all-to-all-start.1 = ((bf16[16,32,256]{2,1,0:T(8,128)(2,1)}), bf16[16,32,256]{2,1,0:T(8,128)(2,1)S(1)}, u32[]{:S(2)}, u32[]{:S(2)}) async-start(bf16[16,32,256]{2,1,0:T(8,128)(2,1)} %bitcast.25), calls=%async_computation.1 | async-start | bytes 524288 | tf_op jit(solution)/shard_map/all_to_all | solution.py:11
  144.7 87.3 %collective-permute-start.8 = (bf16[512,3072]{1,0:T(8,128)(2,1)S(1)}, bf16[512,3072]{1,0:T(8,128)(2,1)}, u32[]{:S(2)}, u32[]{:S(2)}) collective-permute-start(bf16[512,3072]{1,0:T(8,128)(2,1)S(1)} %pad_maximum_fusion.1), channel_id=1, source_target_pairs={{0,64},{16,80},{32,96},{48,112},{64,0},{80,16},{96,32},{112,48},{1... | collective-permute-start | bytes 9437192 | tf_op jit(solution)/shard_map/ppermute | solution.py:35
  227.0 5.0 %collective-permute-start.7 = (bf16[128,512]{1,0:T(8,128)(2,1)S(1)}, bf16[128,512]{1,0:T(8,128)(2,1)S(1)}, u32[]{:S(2)}, u32[]{:S(2)}) collective-permute-start(bf16[128,512]{1,0:T(8,128)(2,1)S(1)} %get-tuple-element.26), channel_id=1, source_target_pairs={{0,64},{16,80},{32,96},{48,112},{64,0},{80,16},{96,32},{112,48},{1... | collective-permute-start | bytes 393224 | tf_op jit(solution)/shard_map/ppermute | solution.py:35
  231.6 4.7 %collective-permute-start.9 = (bf16[128,512]{1,0:T(8,128)(2,1)S(1)}, bf16[128,512]{1,0:T(8,128)(2,1)S(1)}, u32[]{:S(2)}, u32[]{:S(2)}) collective-permute-start(bf16[128,512]{1,0:T(8,128)(2,1)S(1)} %fusion.5), channel_id=1, source_target_pairs={{0,64},{16,80},{32,96},{48,112},{64,0},{80,16},{96,32},{112,48},{1... | collective-permute-start | bytes 393224 | tf_op jit(solution)/shard_map/ppermute | solution.py:35
  241.7 17.9 %all-to-all-start.2 = ((bf16[16,32,256]{2,1,0:T(8,128)(2,1)}), bf16[16,32,256]{2,1,0:T(8,128)(2,1)S(1)}, u32[]{:S(2)}, u32[]{:S(2)}) async-start(bf16[16,32,256]{2,1,0:T(8,128)(2,1)} %bitcast.37), calls=%async_computation.2 | async-start | bytes 524288 | tf_op jit(solution)/shard_map/all_to_all | solution.py:11
  248.0 88.8 %collective-permute-start.11 = (bf16[512,3072]{1,0:T(8,128)(2,1)S(1)}, bf16[512,3072]{1,0:T(8,128)(2,1)}, u32[]{:S(2)}, u32[]{:S(2)}) collective-permute-start(bf16[512,3072]{1,0:T(8,128)(2,1)S(1)} %pad_maximum_fusion.2), channel_id=1, source_target_pairs={{0,128},{16,144},{32,160},{48,176},{64,192},{80,208},{96,224},{112... | collective-permute-start | bytes 9437192 | tf_op jit(solution)/shard_map/ppermute | solution.py:35
  330.4 6.5 %collective-permute-start.10 = (bf16[128,512]{1,0:T(8,128)(2,1)S(1)}, bf16[128,512]{1,0:T(8,128)(2,1)S(1)}, u32[]{:S(2)}, u32[]{:S(2)}) collective-permute-start(bf16[128,512]{1,0:T(8,128)(2,1)S(1)} %get-tuple-element.28), channel_id=1, source_target_pairs={{0,128},{16,144},{32,160},{48,176},{64,192},{80,208},{96,224},{112... | collective-permute-start | bytes 393224 | tf_op jit(solution)/shard_map/ppermute | solution.py:35
  335.6 9.4 %copy-start.7 = (bf16[128,3072]{1,0:T(8,128)(2,1)}, bf16[128,3072]{1,0:T(8,128)(2,1)S(1)}, u32[]{:S(2)}) copy-start(bf16[128,3072]{1,0:T(8,128)(2,1)S(1)} %convolution_convert_fusion.3) | copy-start | bytes 2359300
  336.3 6.2 %collective-permute-start.12 = (bf16[128,512]{1,0:T(8,128)(2,1)S(1)}, bf16[128,512]{1,0:T(8,128)(2,1)S(1)}, u32[]{:S(2)}, u32[]{:S(2)}) collective-permute-start(bf16[128,512]{1,0:T(8,128)(2,1)S(1)} %fusion.6), channel_id=1, source_target_pairs={{0,128},{16,144},{32,160},{48,176},{64,192},{80,208},{96,224},{112... | collective-permute-start | bytes 393224 | tf_op jit(solution)/shard_map/ppermute | solution.py:35
  347.7 17.9 %all-to-all-start.3 = ((bf16[16,32,256]{2,1,0:T(8,128)(2,1)}), bf16[16,32,256]{2,1,0:T(8,128)(2,1)S(1)}, u32[]{:S(2)}, u32[]{:S(2)}) async-start(bf16[16,32,256]{2,1,0:T(8,128)(2,1)} %bitcast.49), calls=%async_computation.3 | async-start | bytes 524288 | tf_op jit(solution)/shard_map/all_to_all | solution.py:11
  354.0 77.0 %copy-start.8 = (bf16[128,3072]{1,0:T(8,128)(2,1)S(1)}, bf16[128,3072]{1,0:T(8,128)(2,1)}, u32[]{:S(2)}) copy-start(bf16[128,3072]{1,0:T(8,128)(2,1)} %copy-done.7) | copy-start | bytes 2359300
  354.0 77.0 %copy-start.10 = (bf16[128,3072]{1,0:T(8,128)(2,1)S(1)}, bf16[128,3072]{1,0:T(8,128)(2,1)}, u32[]{:S(2)}) copy-start(bf16[128,3072]{1,0:T(8,128)(2,1)} %copy-done.9) | copy-start | bytes 2359300
  (7 other events, 20.4 us)

commit v3 on v1

--- a/solution.py
+++ b/solution.py
@@ -74,11 +74,13 @@
         preferred_element_type=jnp.float32,
     )
     half = normal.shape[0] // 2
-    low_11 = jnp.linalg.cholesky(normal[:half, :half])
+    low_11 = lax.linalg.cholesky(normal[:half, :half], symmetrize_input=False)
     low_21 = lax.linalg.triangular_solve(
         low_11, normal[half:, :half], left_side=False, lower=True, transpose_a=True
     )
-    low_22 = jnp.linalg.cholesky(normal[half:, half:] - highest_dot(low_21, low_21.T))
+    low_22 = lax.linalg.cholesky(
+        normal[half:, half:] - highest_dot(low_21, low_21.T), symmetrize_input=False
+    )
     upper_rows = jax.scipy.linalg.solve_triangular(low_11, mixed_cols[:, :half].T, lower=True)
     lower_rows = jax.scipy.linalg.solve_triangular(
         low_22, mixed_cols[:, half:].T - highest_dot(low_21, upper_rows), lower=True

time: 416 us -> 414 us (level)
  transfers between devices with their start and end apart: 14 -> 14, of which waited for: 9 -> 9; matrix products, arithmetic and copies ran while one was open for 40% -> 39% of each run, Pallas kernels for 0% -> 0%
where the time goes in v3:
time: 414 us; the launch traced here: 408 us
  other arithmetic  198 us (48%)
  blocking collectives  64.8 us (16%)
  waiting for transfers between devices  52.9 us (13%)
  starting transfers between devices  50.5 us (12%)
  matrix products  38 us (9%)
    all_gather x4, blocking collectives, summed_rows(): return lax.all_gather(own_rows, axis, axis=0, tiled=True)  64.8 us
    another operation x12, other arithmetic, rotation_of(): low_11 = lax.linalg.cholesky(normal[:half, :half], symmetrize_input=False)  49.6 us
    another operation x12, other arithmetic, rotation_of(): lax.linalg.cholesky(normal[half:, half:] - highest_dot(low_21, low_21.T),...  49.6 us
    another operation x8, other arithmetic, rotation_of(): jax.scipy.linalg.solve_triangular(low_22, mixed_cols[:, half:].T - highes...  42.8 us
    another operation x8, other arithmetic, rotation_of(): jax.scipy.linalg.solve_triangular(low_11, mixed_cols[:, :half].T, lower=T...  41.9 us
    all_to_all x4, waiting for transfers between devices, summed_rows(): parts = lax.all_to_all(shard, axis, 0, 0, tiled=True)  33.7 us
    all_to_all x4, starting transfers between devices, summed_rows(): parts = lax.all_to_all(shard, axis, 0, 0, tiled=True)  27.6 us
    dot_general x7, matrix products, rotated(): jnp.dot(rotation, stacked, preferred_element_type=jnp.float32)  17.9 us
  transfers between devices with their start and end apart: 14, of which 9 were waited for; matrix products, arithmetic and copies ran while one was open for 39% of the time, Pallas kernels for 0%

profile of v3, /device:TPU:1, one launch (start us, length us, event | category | flops | bytes accessed | tf_op | source)
XLA Modules:
  0.0 408.4 jit_solution(4200883872748051215)
XLA Ops:
  27.1 9.4 %all-to-all-start = ((bf16[16,32,256]{2,1,0:T(8,128)(2,1)}), bf16[16,32,256]{2,1,0:T(8,128)(2,1)S(1)}, u32[]{:S(2)}, u32[]{:S(2)}) async-start(bf16[16,32,256]{2,1,0:T(8,128)(2,1)} %bitcast.13), calls=%async_computation | async-start | bytes 524288 | tf_op jit(solution)/shard_map/all_to_all | solution.py:15
  41.2 6.9 %all-to-all-done = bf16[16,32,256]{2,1,0:T(8,128)(2,1)S(1)} async-done(((bf16[16,32,256]{2,1,0:T(8,128)(2,1)}), bf16[16,32,256]{2,1,0:T(8,128)(2,1)S(1)}, u32[]{:S(2)}, u32[]{:S(2)}) %all-to-all-start) | async-done | bytes 262176 | tf_op jit(solution)/shard_map/all_to_all | solution.py:15
  48.1 16.4 %all_gather.12 = f32[512,256]{1,0:T(8,128)S(1)} all-gather(f32[32,256]{1,0:T(8,128)S(1)} %convert_reduce_fusion.4), channel_id=1, replica_groups=mesh['tm'=16,'space'=16] {'space'}, dimensions={0}, use_global_device_ids=true | all-gather | bytes 557056 | tf_op jit(solution)/shard_map/all_gather | solution.py:18
  65.6 11.7 %custom-call.26 = f32[128,128]{1,0:T(8,128)S(1)} custom-call(f32[128,128]{1,0:T(8,128)S(1)} %slice.164), custom_call_target="Cholesky" | custom-call | tf_op jit(solution)/shard_map/cholesky/custom-call.1 | solution.py:77
  78.7 9.8 %custom-call.27 = f32[1,128,128]{1,2,0:T(8,128)S(1)} custom-call(f32[1,128,128]{2,1,0:T(8,128)S(1)} %fusion.27), custom_call_target="InvertDiagBlocksLowerTriangular" | custom-call | tf_op jit(solution)/shard_map/jit(_solve_triangular)/triangular_solve | solution.py:84
  89.1 11.7 %custom-call.29 = f32[128,128]{1,0:T(8,128)S(1)} custom-call(f32[128,128]{1,0:T(8,128)S(1)} %convolution_subtract_fusion.7), custom_call_target="Cholesky" | custom-call | tf_op jit(solution)/shard_map/cholesky/custom-call.1 | solution.py:81
  102.1 9.9 %custom-call.30 = f32[1,128,128]{1,2,0:T(8,128)S(1)} custom-call(f32[1,128,128]{2,1,0:T(8,128)S(1)} %fusion.28), custom_call_target="InvertDiagBlocksLowerTriangular" | custom-call | tf_op jit(solution)/shard_map/jit(_solve_triangular)/triangular_solve | solution.py:85
  137.6 8.4 %all-to-all-done.1 = bf16[16,32,256]{2,1,0:T(8,128)(2,1)S(1)} async-done(((bf16[16,32,256]{2,1,0:T(8,128)(2,1)}), bf16[16,32,256]{2,1,0:T(8,128)(2,1)S(1)}, u32[]{:S(2)}, u32[]{:S(2)}) %all-to-all-start.1) | async-done | bytes 262176 | tf_op jit(solution)/shard_map/all_to_all | solution.py:15
  146.1 16.1 %all_gather.13 = f32[512,256]{1,0:T(8,128)S(1)} all-gather(f32[32,256]{1,0:T(8,128)S(1)} %convert_reduce_fusion.3), channel_id=1, replica_groups=mesh['tm'=16,'space'=16] {'space'}, dimensions={0}, use_global_device_ids=true | all-gather | bytes 557056 | tf_op jit(solution)/shard_map/all_gather | solution.py:18
  163.2 11.7 %custom-call.31 = f32[128,128]{1,0:T(8,128)S(1)} custom-call(f32[128,128]{1,0:T(8,128)S(1)} %slice.171), custom_call_target="Cholesky" | custom-call | tf_op jit(solution)/shard_map/cholesky/custom-call.1 | solution.py:77
  176.3 9.8 %custom-call.32 = f32[1,128,128]{1,2,0:T(8,128)S(1)} custom-call(f32[1,128,128]{2,1,0:T(8,128)S(1)} %fusion.29), custom_call_target="InvertDiagBlocksLowerTriangular" | custom-call | tf_op jit(solution)/shard_map/jit(_solve_triangular)/triangular_solve | solution.py:84
  186.7 11.7 %custom-call.34 = f32[128,128]{1,0:T(8,128)S(1)} custom-call(f32[128,128]{1,0:T(8,128)S(1)} %convolution_subtract_fusion.6), custom_call_target="Cholesky" | custom-call | tf_op jit(solution)/shard_map/cholesky/custom-call.1 | solution.py:81
  199.7 10.2 %custom-call.35 = f32[1,128,128]{1,2,0:T(8,128)S(1)} custom-call(f32[1,128,128]{2,1,0:T(8,128)S(1)} %fusion.30), custom_call_target="InvertDiagBlocksLowerTriangular" | custom-call | tf_op jit(solution)/shard_map/jit(_solve_triangular)/triangular_solve | solution.py:85
  242.4 16.1 %all_gather.14 = f32[512,256]{1,0:T(8,128)S(1)} all-gather(f32[32,256]{1,0:T(8,128)S(1)} %convert_reduce_fusion.2), channel_id=1, replica_groups=mesh['tm'=16,'space'=16] {'space'}, dimensions={0}, use_global_device_ids=true | all-gather | bytes 557056 | tf_op jit(solution)/shard_map/all_gather | solution.py:18
  259.5 11.7 %custom-call.36 = f32[128,128]{1,0:T(8,128)S(1)} custom-call(f32[128,128]{1,0:T(8,128)S(1)} %slice.178), custom_call_target="Cholesky" | custom-call | tf_op jit(solution)/shard_map/cholesky/custom-call.1 | solution.py:77
  272.6 9.8 %custom-call.37 = f32[1,128,128]{1,2,0:T(8,128)S(1)} custom-call(f32[1,128,128]{2,1,0:T(8,128)S(1)} %fusion.31), custom_call_target="InvertDiagBlocksLowerTriangular" | custom-call | tf_op jit(solution)/shard_map/jit(_solve_triangular)/triangular_solve | solution.py:84
  283.0 11.7 %custom-call.39 = f32[128,128]{1,0:T(8,128)S(1)} custom-call(f32[128,128]{1,0:T(8,128)S(1)} %convolution_subtract_fusion.5), custom_call_target="Cholesky" | custom-call | tf_op jit(solution)/shard_map/cholesky/custom-call.1 | solution.py:81
  296.1 10.0 %custom-call.40 = f32[1,128,128]{1,2,0:T(8,128)S(1)} custom-call(f32[1,128,128]{2,1,0:T(8,128)S(1)} %fusion.32), custom_call_target="InvertDiagBlocksLowerTriangular" | custom-call | tf_op jit(solution)/shard_map/jit(_solve_triangular)/triangular_solve | solution.py:85
  328.4 11.6 %all-to-all-done.3 = bf16[16,32,256]{2,1,0:T(8,128)(2,1)S(1)} async-done(((bf16[16,32,256]{2,1,0:T(8,128)(2,1)}), bf16[16,32,256]{2,1,0:T(8,128)(2,1)S(1)}, u32[]{:S(2)}, u32[]{:S(2)}) %all-to-all-start.3) | async-done | bytes 262176 | tf_op jit(solution)/shard_map/all_to_all | solution.py:15
  340.1 16.2 %all_gather.15 = f32[512,256]{1,0:T(8,128)S(1)} all-gather(f32[32,256]{1,0:T(8,128)S(1)} %convert_reduce_fusion.1), channel_id=1, replica_groups=mesh['tm'=16,'space'=16] {'space'}, dimensions={0}, use_global_device_ids=true | all-gather | bytes 557056 | tf_op jit(solution)/shard_map/all_gather | solution.py:18
  357.3 11.7 %custom-call.41 = f32[128,128]{1,0:T(8,128)S(1)} custom-call(f32[128,128]{1,0:T(8,128)S(1)} %slice.185), custom_call_target="Cholesky" | custom-call | tf_op jit(solution)/shard_map/cholesky/custom-call.1 | solution.py:77
  370.3 9.8 %custom-call.42 = f32[1,128,128]{1,2,0:T(8,128)S(1)} custom-call(f32[1,128,128]{2,1,0:T(8,128)S(1)} %fusion.33), custom_call_target="InvertDiagBlocksLowerTriangular" | custom-call | tf_op jit(solution)/shard_map/jit(_solve_triangular)/triangular_solve | solution.py:84
  381.1 11.7 %custom-call.44 = f32[128,128]{1,0:T(8,128)S(1)} custom-call(f32[128,128]{1,0:T(8,128)S(1)} %convolution_subtract_fusion.4), custom_call_target="Cholesky" | custom-call | tf_op jit(solution)/shard_map/cholesky/custom-call.1 | solution.py:81
  394.2 10.1 %custom-call.45 = f32[1,128,128]{1,2,0:T(8,128)S(1)} custom-call(f32[1,128,128]{2,1,0:T(8,128)S(1)} %fusion.34), custom_call_target="InvertDiagBlocksLowerTriangular" | custom-call | tf_op jit(solution)/shard_map/jit(_solve_triangular)/triangular_solve | solution.py:85
  (140 shorter events, 133.0 us)
Async XLA Ops:
  0.0 14.9 %copy-start.3 = (s32[8,128]{1,0:T(8,128)S(1)}, s32[8,128]{1,0:T(8,128)}, u32[]{:S(2)}) copy-start(s32[8,128]{1,0:T(8,128)} %param.12) | copy-start | bytes 12292
  0.0 14.9 %copy-start.4 = (f32[8,128]{1,0:T(8,128)S(1)}, f32[8,128]{1,0:T(8,128)}, u32[]{:S(2)}) copy-start(f32[8,128]{1,0:T(8,128)} %param.11) | copy-start | bytes 12292
  6.1 17.1 %collective-permute-start.2 = (bf16[256,8,128]{0,2,1:T(8,128)(2,1)S(1)}, bf16[256,8,128]{0,2,1:T(8,128)(2,1)S(1)}, u32[]{:S(2)}, u32[]{:S(2)}) collective-permute-start(bf16[256,8,128]{0,2,1:T(8,128)(2,1)S(1)} %multiply_convert_fusion), channel_id=1, source_target_pairs={{0,16},{16,0},{32,48},{48,32},{64,80},{80,64},{96,112},{112,96},{1... | collective-permute-start | bytes 1572872 | tf_op jit(solution)/shard_map/ppermute | solution.py:39
  8.2 7.2 %collective-permute-start = (bf16[256,1,128]{0,2,1:T(8,128)(2,1)S(1)}, bf16[256,1,128]{0,2,1:T(8,128)(2,1)S(1)}, u32[]{:S(2)}, u32[]{:S(2)}) collective-permute-start(bf16[256,1,128]{0,2,1:T(8,128)(2,1)S(1)} %get-tuple-element.6), channel_id=1, source_target_pairs={{0,1},{1,2},{2,3},{3,4},{4,5},{5,6},{6,7},{7,8},{8,9},{9,10},{10,1... | collective-permute-start | bytes 196616 | tf_op jit(solution)/shard_map/ppermute | solution.py:29
  12.6 5.9 %collective-permute-start.1 = (bf16[256,1,128]{0,2,1:T(8,128)(2,1)S(1)}, bf16[256,1,128]{0,2,1:T(8,128)(2,1)S(1)}, u32[]{:S(2)}, u32[]{:S(2)}) collective-permute-start(bf16[256,1,128]{0,2,1:T(8,128)(2,1)S(1)} %get-tuple-element.8), channel_id=1, source_target_pairs={{1,0},{2,1},{3,2},{4,3},{5,4},{6,5},{7,6},{8,7},{9,8},{10,9},{11,1... | collective-permute-start | bytes 196616 | tf_op jit(solution)/shard_map/ppermute | solution.py:31
  18.5 4.7 %collective-permute-start.3 = (bf16[256,2,128]{0,2,1:T(8,128)(2,1)S(1)}, bf16[256,2,128]{0,2,1:T(8,128)(2,1)S(1)}, u32[]{:S(2)}, u32[]{:S(2)}) collective-permute-start(bf16[256,2,128]{0,2,1:T(8,128)(2,1)S(1)} %pad_maximum_fusion.10), channel_id=1, source_target_pairs={{0,16},{16,0},{32,48},{48,32},{64,80},{80,64},{96,112},{112,96},{1... | collective-permute-start | bytes 393224 | tf_op jit(solution)/shard_map/ppermute | solution.py:39
  24.5 12.0 %copy-start = (bf16[256,3,8,128]{0,3,2,1:T(8,128)(2,1)}, bf16[256,3,8,128]{0,3,2,1:T(8,128)(2,1)S(1)}, u32[]{:S(2)}) copy-start(bf16[256,3,8,128]{0,3,2,1:T(8,128)(2,1)S(1)} %get-tuple-element.17) | copy-start | bytes 4718596
  27.1 21.0 %all-to-all-start = ((bf16[16,32,256]{2,1,0:T(8,128)(2,1)}), bf16[16,32,256]{2,1,0:T(8,128)(2,1)S(1)}, u32[]{:S(2)}, u32[]{:S(2)}) async-start(bf16[16,32,256]{2,1,0:T(8,128)(2,1)} %bitcast.13), calls=%async_computation | async-start | bytes 524288 | tf_op jit(solution)/shard_map/all_to_all | solution.py:15
  38.4 84.4 %collective-permute-start.5 = (bf16[512,3072]{0,1:T(8,128)(2,1)}, bf16[512,3072]{0,1:T(8,128)(2,1)}, u32[]{:S(2)}, u32[]{:S(2)}) collective-permute-start(bf16[512,3072]{0,1:T(8,128)(2,1)} %pad_maximum_fusion), channel_id=1, source_target_pairs={{0,32},{16,48},{32,0},{48,16},{64,96},{80,112},{96,64},{112,80},{1... | collective-permute-start | bytes 9437192 | tf_op jit(solution)/shard_map/ppermute | solution.py:39
  113.6 9.3 %collective-permute-start.4 = (bf16[256,512]{1,0:T(8,128)(2,1)S(1)}, bf16[256,512]{1,0:T(8,128)(2,1)S(1)}, u32[]{:S(2)}, u32[]{:S(2)}) collective-permute-start(bf16[256,512]{1,0:T(8,128)(2,1)S(1)} %fusion.20), channel_id=1, source_target_pairs={{0,32},{16,48},{32,0},{48,16},{64,96},{80,112},{96,64},{112,80},{1... | collective-permute-start | bytes 786440 | tf_op jit(solution)/shard_map/ppermute | solution.py:39
  118.8 15.6 %copy-start.1 = (bf16[256,3072]{1,0:T(8,128)(2,1)}, bf16[256,3072]{1,0:T(8,128)(2,1)S(1)}, u32[]{:S(2)}) copy-start(bf16[256,3072]{1,0:T(8,128)(2,1)S(1)} %convolution_convert_fusion.5) | copy-start | bytes 4718596
  128.4 17.7 %all-to-all-start.1 = ((bf16[16,32,256]{2,1,0:T(8,128)(2,1)}), bf16[16,32,256]{2,1,0:T(8,128)(2,1)S(1)}, u32[]{:S(2)}, u32[]{:S(2)}) async-start(bf16[16,32,256]{2,1,0:T(8,128)(2,1)} %bitcast.23), calls=%async_computation.1 | async-start | bytes 524288 | tf_op jit(solution)/shard_map/all_to_all | solution.py:15
  136.3 82.9 %collective-permute-start.7 = (bf16[512,3072]{1,0:T(8,128)(2,1)}, bf16[512,3072]{1,0:T(8,128)(2,1)}, u32[]{:S(2)}, u32[]{:S(2)}) collective-permute-start(bf16[512,3072]{1,0:T(8,128)(2,1)} %pad_maximum_fusion.1), channel_id=1, source_target_pairs={{0,64},{16,80},{32,96},{48,112},{64,0},{80,16},{96,32},{112,48},{1... | collective-permute-start | bytes 9437192 | tf_op jit(solution)/shard_map/ppermute | solution.py:39
  211.4 7.8 %collective-permute-start.6 = (bf16[256,512]{1,0:T(8,128)(2,1)S(1)}, bf16[256,512]{1,0:T(8,128)(2,1)S(1)}, u32[]{:S(2)}, u32[]{:S(2)}) collective-permute-start(bf16[256,512]{1,0:T(8,128)(2,1)S(1)} %fusion.21), channel_id=1, source_target_pairs={{0,64},{16,80},{32,96},{48,112},{64,0},{80,16},{96,32},{112,48},{1... | collective-permute-start | bytes 786440 | tf_op jit(solution)/shard_map/ppermute | solution.py:39
  215.2 15.5 %copy-start.2 = (bf16[256,3072]{1,0:T(8,128)(2,1)}, bf16[256,3072]{1,0:T(8,128)(2,1)S(1)}, u32[]{:S(2)}) copy-start(bf16[256,3072]{1,0:T(8,128)(2,1)S(1)} %convolution_convert_fusion.3) | copy-start | bytes 4718596
  224.7 17.6 %all-to-all-start.2 = ((bf16[16,32,256]{2,1,0:T(8,128)(2,1)}), bf16[16,32,256]{2,1,0:T(8,128)(2,1)S(1)}, u32[]{:S(2)}, u32[]{:S(2)}) async-start(bf16[16,32,256]{2,1,0:T(8,128)(2,1)} %bitcast.33), calls=%async_computation.2 | async-start | bytes 524288 | tf_op jit(solution)/shard_map/all_to_all | solution.py:15
  232.7 84.2 %collective-permute-start.9 = (bf16[512,3072]{1,0:T(8,128)(2,1)}, bf16[512,3072]{1,0:T(8,128)(2,1)}, u32[]{:S(2)}, u32[]{:S(2)}) collective-permute-start(bf16[512,3072]{1,0:T(8,128)(2,1)} %pad_maximum_fusion.2), channel_id=1, source_target_pairs={{0,128},{16,144},{32,160},{48,176},{64,192},{80,208},{96,224},{112... | collective-permute-start | bytes 9437192 | tf_op jit(solution)/shard_map/ppermute | solution.py:39
  307.5 9.3 %collective-permute-start.8 = (bf16[256,512]{1,0:T(8,128)(2,1)S(1)}, bf16[256,512]{1,0:T(8,128)(2,1)S(1)}, u32[]{:S(2)}, u32[]{:S(2)}) collective-permute-start(bf16[256,512]{1,0:T(8,128)(2,1)S(1)} %fusion.22), channel_id=1, source_target_pairs={{0,128},{16,144},{32,160},{48,176},{64,192},{80,208},{96,224},{112... | collective-permute-start | bytes 786440 | tf_op jit(solution)/shard_map/ppermute | solution.py:39
  312.9 8.7 %copy-start.5 = (bf16[256,3072]{1,0:T(8,128)(2,1)}, bf16[256,3072]{1,0:T(8,128)(2,1)S(1)}, u32[]{:S(2)}) copy-start(bf16[256,3072]{1,0:T(8,128)(2,1)S(1)} %convolution_convert_fusion.1) | copy-start | bytes 4718596
  322.4 17.7 %all-to-all-start.3 = ((bf16[16,32,256]{2,1,0:T(8,128)(2,1)}), bf16[16,32,256]{2,1,0:T(8,128)(2,1)S(1)}, u32[]{:S(2)}, u32[]{:S(2)}) async-start(bf16[16,32,256]{2,1,0:T(8,128)(2,1)} %bitcast.43), calls=%async_computation.3 | async-start | bytes 524288 | tf_op jit(solution)/shard_map/all_to_all | solution.py:15

commit v4 on v3

--- a/solution.py
+++ b/solution.py
@@ -62,10 +62,13 @@
     return jnp.concatenate([own_basis, other_basis], axis=0)
 
 
-def rotation_of(stacked):
-    members = stacked.shape[0] // 2
-    local_gram = jnp.dot(stacked, stacked.T, preferred_element_type=jnp.float32)
-    local_mixed = (local_gram[:, :members] + local_gram[:, members:]) * inv_root2
+def rotation_of(own_basis, other_basis):
+    own_own = jnp.dot(own_basis, own_basis.T, preferred_element_type=jnp.float32)
+    own_other = jnp.dot(own_basis, other_basis.T, preferred_element_type=jnp.float32)
+    other_other = jnp.dot(other_basis, other_basis.T, preferred_element_type=jnp.float32)
+    local_mixed = (
+        jnp.concatenate([own_own + own_other, own_other.T + other_other], axis=0) * inv_root2
+    )
     mixed_cols = summed_rows(local_mixed.astype(jnp.bfloat16), "space")
     normal = jnp.dot(
         mixed_cols.T,
@@ -117,7 +120,7 @@
     stacked = stack_pair(basis_now, partner)
     for level_idx in range(levels):
         if level_idx == levels - 1:
-            rotation = rotation_of(stacked)
+            rotation = rotation_of(basis_now, partner)
             member_share = rotation.shape[0] // lax.axis_size("tm")
             rotation = lax.dynamic_slice_in_dim(
                 rotation, lax.axis_index("tm") * member_share, member_share, 0
@@ -125,7 +128,7 @@
             basis_now = rotated(rotation, stacked)
         else:
             partner_stacked = from_partner(stacked, "tm", level_idx + 1)
-            rotation = rotation_of(stacked)
+            rotation = rotation_of(basis_now, partner)
             partner_rotation = from_partner(rotation, "tm", level_idx + 1)
             basis_now = rotated(rotation, stacked)
             partner = rotated(partner_rotation, partner_stacked)

time: 414 us -> 439 us (1.060)
  other arithmetic: 198 us -> 205 us
  matrix products: 38 us -> 44.5 us
  local copies, waits for them, and re-layouts: 2.95 us -> 9.32 us
    dot_general x8, matrix products: 3.5 us -> 9.09 us  [highest_dot(): jnp.dot(left, right, precision=lax.Precision.HIGHEST, preferred_element_t...]
    dot_general x7, matrix products: 17.9 us -> 12.3 us  [rotated(): jnp.dot(rotation, stacked, preferred_element_type=jnp.float32)]
    another operation x8, other arithmetic: 41.9 us -> 46.3 us  [rotation_of(): jax.scipy.linalg.solve_triangular(low_11, mixed_cols[:, :half].T, lower=T...]
    dot_general x4 -> x12, matrix products: 7.28 us -> 10.8 us  [the longest x4 4.48 us: rotation_of(): jnp.dot(other_basis, other_basis.T, preferred_element_type=jnp.float32)]
where the time goes in v4:
time: 439 us; the launch traced here: 432 us
  other arithmetic  205 us (47%)
  blocking collectives  64.6 us (15%)
  waiting for transfers between devices  56.7 us (13%)
  starting transfers between devices  50.6 us (12%)
  matrix products  44.5 us (10%)
  local copies, waits for them, and re-layouts  9.32 us (2%)
    all_gather x4, blocking collectives, summed_rows(): return lax.all_gather(own_rows, axis, axis=0, tiled=True)  64.6 us
    another operation x12, other arithmetic, rotation_of(): lax.linalg.cholesky(normal[half:, half:] - highest_dot(low_21, low_21.T),...  52.1 us
    another operation x12, other arithmetic, rotation_of(): low_11 = lax.linalg.cholesky(normal[:half, :half], symmetrize_input=False)  49.8 us
    another operation x8, other arithmetic, rotation_of(): jax.scipy.linalg.solve_triangular(low_11, mixed_cols[:, :half].T, lower=T...  46.3 us
    another operation x8, other arithmetic, rotation_of(): jax.scipy.linalg.solve_triangular(low_22, mixed_cols[:, half:].T - highes...  44 us
    all_to_all x4, waiting for transfers between devices, summed_rows(): parts = lax.all_to_all(shard, axis, 0, 0, tiled=True)  33.3 us
    all_to_all x4, starting transfers between devices, summed_rows(): parts = lax.all_to_all(shard, axis, 0, 0, tiled=True)  27.6 us
    ppermute x8, waiting for transfers between devices, from_partner(): lax.ppermute(shard, axis, [(i, i ^ 1 << stride) for i in range(lax.axis_s...  20.3 us
  transfers between devices with their start and end apart: 14, of which 9 were waited for; matrix products, arithmetic and copies ran while one was open for 39% of the time, Pallas kernels for 0%

profile of v4, /device:TPU:1, one launch (start us, length us, event | category | flops | bytes accessed | tf_op | source)
XLA Modules:
  0.0 431.9 jit_solution(3135825528376759553)
XLA Ops:
  28.5 9.4 %all-to-all-start = ((bf16[16,32,256]{2,1,0:T(8,128)(2,1)}), bf16[16,32,256]{2,1,0:T(8,128)(2,1)S(1)}, u32[]{:S(2)}, u32[]{:S(2)}) async-start(bf16[16,32,256]{2,1,0:T(8,128)(2,1)} %bitcast.19), calls=%async_computation | async-start | bytes 524288 | tf_op jit(solution)/shard_map/all_to_all | solution.py:15
  49.5 16.1 %all_gather.12 = f32[512,256]{1,0:T(8,128)S(1)} all-gather(f32[32,256]{1,0:T(8,128)S(1)} %convert_reduce_fusion.4), channel_id=1, replica_groups=mesh['tm'=16,'space'=16] {'space'}, dimensions={0}, use_global_device_ids=true | all-gather | bytes 557056 | tf_op jit(solution)/shard_map/all_gather | solution.py:18
  66.7 11.7 %custom-call.26 = f32[128,128]{1,0:T(8,128)S(1)} custom-call(f32[128,128]{1,0:T(8,128)S(1)} %slice.130), custom_call_target="Cholesky" | custom-call | tf_op jit(solution)/shard_map/cholesky/custom-call.1 | solution.py:80
  79.7 9.8 %custom-call.27 = f32[1,128,128]{1,2,0:T(8,128)S(1)} custom-call(f32[1,128,128]{2,1,0:T(8,128)S(1)} %fusion.28), custom_call_target="InvertDiagBlocksLowerTriangular" | custom-call | tf_op jit(solution)/shard_map/jit(_solve_triangular)/triangular_solve | solution.py:87
  90.1 11.7 %custom-call.29 = f32[128,128]{1,0:T(8,128)S(1)} custom-call(f32[128,128]{1,0:T(8,128)S(1)} %convolution_subtract_fusion.7), custom_call_target="Cholesky" | custom-call | tf_op jit(solution)/shard_map/cholesky/custom-call.1 | solution.py:84
  103.2 10.0 %custom-call.30 = f32[1,128,128]{1,2,0:T(8,128)S(1)} custom-call(f32[1,128,128]{2,1,0:T(8,128)S(1)} %fusion.29), custom_call_target="InvertDiagBlocksLowerTriangular" | custom-call | tf_op jit(solution)/shard_map/jit(_solve_triangular)/triangular_solve | solution.py:88
  141.2 8.4 %all-to-all-done.1 = bf16[16,32,256]{2,1,0:T(8,128)(2,1)S(1)} async-done(((bf16[16,32,256]{2,1,0:T(8,128)(2,1)}), bf16[16,32,256]{2,1,0:T(8,128)(2,1)S(1)}, u32[]{:S(2)}, u32[]{:S(2)}) %all-to-all-start.1) | async-done | bytes 262176 | tf_op jit(solution)/shard_map/all_to_all | solution.py:15
  149.7 16.3 %all_gather.13 = f32[512,256]{1,0:T(8,128)S(1)} all-gather(f32[32,256]{1,0:T(8,128)S(1)} %convert_reduce_fusion.3), channel_id=1, replica_groups=mesh['tm'=16,'space'=16] {'space'}, dimensions={0}, use_global_device_ids=true | all-gather | bytes 557056 | tf_op jit(solution)/shard_map/all_gather | solution.py:18
  167.9 11.7 %custom-call.31 = f32[128,128]{1,0:T(8,128)S(1)} custom-call(f32[128,128]{1,0:T(8,128)S(1)} %slice.135), custom_call_target="Cholesky" | custom-call | tf_op jit(solution)/shard_map/cholesky/custom-call.1 | solution.py:80
  181.7 10.6 %custom-call.32 = f32[1,128,128]{1,2,0:T(8,128)S(1)} custom-call(f32[1,128,128]{2,1,0:T(8,128)} %fusion.30), custom_call_target="InvertDiagBlocksLowerTriangular" | custom-call | tf_op jit(solution)/shard_map/jit(_solve_triangular)/triangular_solve | solution.py:87
  193.5 12.5 %custom-call.34 = f32[128,128]{1,0:T(8,128)S(1)} custom-call(f32[128,128]{1,0:T(8,128)} %convolution_subtract_fusion.6), custom_call_target="Cholesky" | custom-call | tf_op jit(solution)/shard_map/cholesky/custom-call.1 | solution.py:84
  207.4 10.0 %custom-call.35 = f32[1,128,128]{1,2,0:T(8,128)S(1)} custom-call(f32[1,128,128]{2,1,0:T(8,128)S(1)} %fusion.31), custom_call_target="InvertDiagBlocksLowerTriangular" | custom-call | tf_op jit(solution)/shard_map/jit(_solve_triangular)/triangular_solve | solution.py:88
  246.9 6.8 %all-to-all-done.2 = bf16[16,32,256]{2,1,0:T(8,128)(2,1)S(1)} async-done(((bf16[16,32,256]{2,1,0:T(8,128)(2,1)}), bf16[16,32,256]{2,1,0:T(8,128)(2,1)S(1)}, u32[]{:S(2)}, u32[]{:S(2)}) %all-to-all-start.2) | async-done | bytes 262176 | tf_op jit(solution)/shard_map/all_to_all | solution.py:15
  253.7 16.3 %all_gather.14 = f32[512,256]{1,0:T(8,128)S(1)} all-gather(f32[32,256]{1,0:T(8,128)S(1)} %convert_reduce_fusion.2), channel_id=1, replica_groups=mesh['tm'=16,'space'=16] {'space'}, dimensions={0}, use_global_device_ids=true | all-gather | bytes 557056 | tf_op jit(solution)/shard_map/all_gather | solution.py:18
  271.9 11.7 %custom-call.36 = f32[128,128]{1,0:T(8,128)S(1)} custom-call(f32[128,128]{1,0:T(8,128)S(1)} %slice.140), custom_call_target="Cholesky" | custom-call | tf_op jit(solution)/shard_map/cholesky/custom-call.1 | solution.py:80
  285.7 10.6 %custom-call.37 = f32[1,128,128]{1,2,0:T(8,128)S(1)} custom-call(f32[1,128,128]{2,1,0:T(8,128)} %fusion.32), custom_call_target="InvertDiagBlocksLowerTriangular" | custom-call | tf_op jit(solution)/shard_map/jit(_solve_triangular)/triangular_solve | solution.py:87
  297.5 12.5 %custom-call.39 = f32[128,128]{1,0:T(8,128)S(1)} custom-call(f32[128,128]{1,0:T(8,128)} %convolution_subtract_fusion.5), custom_call_target="Cholesky" | custom-call | tf_op jit(solution)/shard_map/cholesky/custom-call.1 | solution.py:84
  311.4 9.9 %custom-call.40 = f32[1,128,128]{1,2,0:T(8,128)S(1)} custom-call(f32[1,128,128]{2,1,0:T(8,128)S(1)} %fusion.33), custom_call_target="InvertDiagBlocksLowerTriangular" | custom-call | tf_op jit(solution)/shard_map/jit(_solve_triangular)/triangular_solve | solution.py:88
  345.8 11.6 %all-to-all-done.3 = bf16[16,32,256]{2,1,0:T(8,128)(2,1)S(1)} async-done(((bf16[16,32,256]{2,1,0:T(8,128)(2,1)}), bf16[16,32,256]{2,1,0:T(8,128)(2,1)S(1)}, u32[]{:S(2)}, u32[]{:S(2)}) %all-to-all-start.3) | async-done | bytes 262176 | tf_op jit(solution)/shard_map/all_to_all | solution.py:15
  357.4 15.9 %all_gather.15 = f32[512,256]{1,0:T(8,128)S(1)} all-gather(f32[32,256]{1,0:T(8,128)S(1)} %convert_reduce_fusion.1), channel_id=1, replica_groups=mesh['tm'=16,'space'=16] {'space'}, dimensions={0}, use_global_device_ids=true | all-gather | bytes 557056 | tf_op jit(solution)/shard_map/all_gather | solution.py:18
  375.2 11.7 %custom-call.41 = f32[128,128]{1,0:T(8,128)S(1)} custom-call(f32[128,128]{1,0:T(8,128)S(1)} %slice.145), custom_call_target="Cholesky" | custom-call | tf_op jit(solution)/shard_map/cholesky/custom-call.1 | solution.py:80
  388.9 10.6 %custom-call.42 = f32[1,128,128]{1,2,0:T(8,128)S(1)} custom-call(f32[1,128,128]{2,1,0:T(8,128)} %fusion.34), custom_call_target="InvertDiagBlocksLowerTriangular" | custom-call | tf_op jit(solution)/shard_map/jit(_solve_triangular)/triangular_solve | solution.py:87
  403.0 12.5 %custom-call.44 = f32[128,128]{1,0:T(8,128)S(1)} custom-call(f32[128,128]{1,0:T(8,128)} %convolution_subtract_fusion.4), custom_call_target="Cholesky" | custom-call | tf_op jit(solution)/shard_map/cholesky/custom-call.1 | solution.py:84
  417.7 10.8 %custom-call.45 = f32[1,128,128]{1,2,0:T(8,128)S(1)} custom-call(f32[1,128,128]{2,1,0:T(8,128)} %fusion.35), custom_call_target="InvertDiagBlocksLowerTriangular" | custom-call | tf_op jit(solution)/shard_map/jit(_solve_triangular)/triangular_solve | solution.py:88
  (170 shorter events, 151.4 us)
Async XLA Ops:
  0.0 4.4 %copy-start.15 = (s32[1,256]{1,0:T(1,128)S(1)}, s32[1,256]{1,0:T(1,128)}, u32[]{:S(2)}) copy-start(s32[1,256]{1,0:T(1,128)} %param.10) | copy-start | bytes 3076
  0.0 4.4 %copy-start.13 = (s32[8,128]{1,0:T(8,128)S(1)}, s32[8,128]{1,0:T(8,128)}, u32[]{:S(2)}) copy-start(s32[8,128]{1,0:T(8,128)} %param.12) | copy-start | bytes 12292
  4.0 9.6 %copy-start.14 = (f32[8,128]{1,0:T(8,128)S(1)}, f32[8,128]{1,0:T(8,128)}, u32[]{:S(2)}) copy-start(f32[8,128]{1,0:T(8,128)} %param.11) | copy-start | bytes 12292
  4.8 17.1 %collective-permute-start.2 = (bf16[256,8,128]{0,2,1:T(8,128)(2,1)S(1)}, bf16[256,8,128]{0,2,1:T(8,128)(2,1)S(1)}, u32[]{:S(2)}, u32[]{:S(2)}) collective-permute-start(bf16[256,8,128]{0,2,1:T(8,128)(2,1)S(1)} %multiply_convert_fusion), channel_id=1, source_target_pairs={{0,16},{16,0},{32,48},{48,32},{64,80},{80,64},{96,112},{112,96},{1... | collective-permute-start | bytes 1572872 | tf_op jit(solution)/shard_map/ppermute | solution.py:39
  6.9 7.2 %collective-permute-start = (bf16[256,1,128]{0,2,1:T(8,128)(2,1)S(1)}, bf16[256,1,128]{0,2,1:T(8,128)(2,1)S(1)}, u32[]{:S(2)}, u32[]{:S(2)}) collective-permute-start(bf16[256,1,128]{0,2,1:T(8,128)(2,1)S(1)} %get-tuple-element.6), channel_id=1, source_target_pairs={{0,1},{1,2},{2,3},{3,4},{4,5},{5,6},{6,7},{7,8},{8,9},{9,10},{10,1... | collective-permute-start | bytes 196616 | tf_op jit(solution)/shard_map/ppermute | solution.py:29
  11.3 5.9 %collective-permute-start.1 = (bf16[256,1,128]{0,2,1:T(8,128)(2,1)S(1)}, bf16[256,1,128]{0,2,1:T(8,128)(2,1)S(1)}, u32[]{:S(2)}, u32[]{:S(2)}) collective-permute-start(bf16[256,1,128]{0,2,1:T(8,128)(2,1)S(1)} %get-tuple-element.8), channel_id=1, source_target_pairs={{1,0},{2,1},{3,2},{4,3},{5,4},{6,5},{7,6},{8,7},{9,8},{10,9},{11,1... | collective-permute-start | bytes 196616 | tf_op jit(solution)/shard_map/ppermute | solution.py:31
  17.2 4.7 %collective-permute-start.3 = (bf16[256,2,128]{0,2,1:T(8,128)(2,1)S(1)}, bf16[256,2,128]{0,2,1:T(8,128)(2,1)S(1)}, u32[]{:S(2)}, u32[]{:S(2)}) collective-permute-start(bf16[256,2,128]{0,2,1:T(8,128)(2,1)S(1)} %pad_maximum_fusion.5), channel_id=1, source_target_pairs={{0,16},{16,0},{32,48},{48,32},{64,80},{80,64},{96,112},{112,96},{1... | collective-permute-start | bytes 393224 | tf_op jit(solution)/shard_map/ppermute | solution.py:39
  28.5 21.0 %all-to-all-start = ((bf16[16,32,256]{2,1,0:T(8,128)(2,1)}), bf16[16,32,256]{2,1,0:T(8,128)(2,1)S(1)}, u32[]{:S(2)}, u32[]{:S(2)}) async-start(bf16[16,32,256]{2,1,0:T(8,128)(2,1)} %bitcast.19), calls=%async_computation | async-start | bytes 524288 | tf_op jit(solution)/shard_map/all_to_all | solution.py:15
  38.1 2.2 copy-start.7
  40.2 83.7 %collective-permute-start.5 = (bf16[512,3072]{0,1:T(8,128)(2,1)}, bf16[512,3072]{0,1:T(8,128)(2,1)}, u32[]{:S(2)}, u32[]{:S(2)}) collective-permute-start(bf16[512,3072]{0,1:T(8,128)(2,1)} %pad_maximum_fusion), channel_id=1, source_target_pairs={{0,32},{16,48},{32,0},{48,16},{64,96},{80,112},{96,64},{112,80},{1... | collective-permute-start | bytes 9437192 | tf_op jit(solution)/shard_map/ppermute | solution.py:39
  113.2 4.3 %copy-start.8 = (bf16[256,3,8,128]{0,3,2,1:T(8,128)(2,1)S(1)}, bf16[256,3,8,128]{0,3,2,1:T(8,128)(2,1)}, u32[]{:S(2)}) copy-start(bf16[256,3,8,128]{0,3,2,1:T(8,128)(2,1)} %copy-done.7) | copy-start | bytes 4718596
  114.7 9.3 %collective-permute-start.4 = (bf16[256,512]{1,0:T(8,128)(2,1)S(1)}, bf16[256,512]{1,0:T(8,128)(2,1)S(1)}, u32[]{:S(2)}, u32[]{:S(2)}) collective-permute-start(bf16[256,512]{1,0:T(8,128)(2,1)S(1)} %fusion.18), channel_id=1, source_target_pairs={{0,32},{16,48},{32,0},{48,16},{64,96},{80,112},{96,64},{112,80},{1... | collective-permute-start | bytes 786440 | tf_op jit(solution)/shard_map/ppermute | solution.py:39
  132.0 17.7 %all-to-all-start.1 = ((bf16[16,32,256]{2,1,0:T(8,128)(2,1)}), bf16[16,32,256]{2,1,0:T(8,128)(2,1)S(1)}, u32[]{:S(2)}, u32[]{:S(2)}) async-start(bf16[16,32,256]{2,1,0:T(8,128)(2,1)} %bitcast.32), calls=%async_computation.1 | async-start | bytes 524288 | tf_op jit(solution)/shard_map/all_to_all | solution.py:15
  139.9 88.7 %collective-permute-start.7 = (bf16[512,3072]{1,0:T(8,128)(2,1)}, bf16[512,3072]{1,0:T(8,128)(2,1)}, u32[]{:S(2)}, u32[]{:S(2)}) collective-permute-start(bf16[512,3072]{1,0:T(8,128)(2,1)} %pad_maximum_fusion.1), channel_id=1, source_target_pairs={{0,64},{16,80},{32,96},{48,112},{64,0},{80,16},{96,32},{112,48},{1... | collective-permute-start | bytes 9437192 | tf_op jit(solution)/shard_map/ppermute | solution.py:39
  220.8 7.8 %collective-permute-start.6 = (bf16[256,512]{1,0:T(8,128)(2,1)S(1)}, bf16[256,512]{1,0:T(8,128)(2,1)S(1)}, u32[]{:S(2)}, u32[]{:S(2)}) collective-permute-start(bf16[256,512]{1,0:T(8,128)(2,1)S(1)} %fusion.20), channel_id=1, source_target_pairs={{0,64},{16,80},{32,96},{48,112},{64,0},{80,16},{96,32},{112,48},{1... | collective-permute-start | bytes 786440 | tf_op jit(solution)/shard_map/ppermute | solution.py:39
  223.2 8.9 %copy-start = (bf16[256,3072]{1,0:T(8,128)(2,1)}, bf16[256,3072]{1,0:T(8,128)(2,1)S(1)}, u32[]{:S(2)}) copy-start(bf16[256,3072]{1,0:T(8,128)(2,1)S(1)} %convolution_convert_fusion.3) | copy-start | bytes 4718596
  233.6 8.5 %copy-start.1 = (bf16[256,3072]{1,0:T(8,128)(2,1)S(1)}, bf16[256,3072]{1,0:T(8,128)(2,1)}, u32[]{:S(2)}) copy-start(bf16[256,3072]{1,0:T(8,128)(2,1)} %copy-done) | copy-start | bytes 4718596
  236.0 17.6 %all-to-all-start.2 = ((bf16[16,32,256]{2,1,0:T(8,128)(2,1)}), bf16[16,32,256]{2,1,0:T(8,128)(2,1)S(1)}, u32[]{:S(2)}, u32[]{:S(2)}) async-start(bf16[16,32,256]{2,1,0:T(8,128)(2,1)} %bitcast.213), calls=%async_computation.2 | async-start | bytes 524288 | tf_op jit(solution)/shard_map/all_to_all | solution.py:15
  243.9 90.1 %collective-permute-start.9 = (bf16[512,3072]{1,0:T(8,128)(2,1)}, bf16[512,3072]{1,0:T(8,128)(2,1)}, u32[]{:S(2)}, u32[]{:S(2)}) collective-permute-start(bf16[512,3072]{1,0:T(8,128)(2,1)} %pad_maximum_fusion.2), channel_id=1, source_target_pairs={{0,128},{16,144},{32,160},{48,176},{64,192},{80,208},{96,224},{112... | collective-permute-start | bytes 9437192 | tf_op jit(solution)/shard_map/ppermute | solution.py:39
  324.8 9.3 %collective-permute-start.8 = (bf16[256,512]{1,0:T(8,128)(2,1)S(1)}, bf16[256,512]{1,0:T(8,128)(2,1)S(1)}, u32[]{:S(2)}, u32[]{:S(2)}) collective-permute-start(bf16[256,512]{1,0:T(8,128)(2,1)S(1)} %fusion.22), channel_id=1, source_target_pairs={{0,128},{16,144},{32,160},{48,176},{64,192},{80,208},{96,224},{112... | collective-permute-start | bytes 786440 | tf_op jit(solution)/shard_map/ppermute | solution.py:39
  328.8 8.8 %copy-start.2 = (bf16[256,3072]{1,0:T(8,128)(2,1)}, bf16[256,3072]{1,0:T(8,128)(2,1)S(1)}, u32[]{:S(2)}) copy-start(bf16[256,3072]{1,0:T(8,128)(2,1)S(1)} %convolution_convert_fusion.1) | copy-start | bytes 4718596
  339.7 17.7 %all-to-all-start.3 = ((bf16[16,32,256]{2,1,0:T(8,128)(2,1)}), bf16[16,32,256]{2,1,0:T(8,128)(2,1)S(1)}, u32[]{:S(2)}, u32[]{:S(2)}) async-start(bf16[16,32,256]{2,1,0:T(8,128)(2,1)} %bitcast.54), calls=%async_computation.3 | async-start | bytes 524288 | tf_op jit(solution)/shard_map/all_to_all | solution.py:15
  375.2 24.4 %copy-start.10 = (f32[256,256]{1,0:T(8,128)}, f32[256,256]{1,0:T(8,128)S(1)}, u32[]{:S(2)}) copy-start(f32[256,256]{1,0:T(8,128)S(1)} %fusion.90) | copy-start | bytes 786436
  375.2 55.3 %copy-start.3 = (bf16[256,3072]{1,0:T(8,128)(2,1)S(1)}, bf16[256,3072]{1,0:T(8,128)(2,1)}, u32[]{:S(2)}) copy-start(bf16[256,3072]{1,0:T(8,128)(2,1)} %copy-done.2) | copy-start | bytes 4718596
  (6 other events, 5.7 us)

commit v5 on v3

--- a/solution.py
+++ b/solution.py
@@ -15,7 +15,17 @@
     parts = lax.all_to_all(shard, axis, 0, 0, tiled=True)
     parts = parts.reshape(count, shard.shape[0] // count, shard.shape[1])
     own_rows = parts.astype(jnp.float32).sum(0)
-    return lax.all_gather(own_rows, axis, axis=0, tiled=True)
+    index = lax.axis_index(axis)
+    step = 1
+    while step < count:
+        other = lax.ppermute(own_rows, axis, [(i, i ^ step) for i in range(count)])
+        own_rows = jnp.where(
+            index // step % 2 == 0,
+            jnp.concatenate([own_rows, other], axis=0),
+            jnp.concatenate([other, own_rows], axis=0),
+        )
+        step *= 2
+    return own_rows
 
 
 def with_halo(cells, sides, width):

time: 414 us -> 487 us (1.18)
  waiting for transfers between devices: 52.9 us -> 132 us
  starting transfers between devices: 50.5 us -> 25.3 us
  blocking collectives: 64.8 us -> 82.4 us
    ppermute x0 -> x16, waiting for transfers between devices: none -> 97.9 us  [summed_rows(): other = lax.ppermute(own_rows, axis, [(i, i ^ step) for i in range(count)])]
    all_to_all x0 -> x4, blocking collectives: none -> 82.4 us  [summed_rows(): parts = lax.all_to_all(shard, axis, 0, 0, tiled=True)]
    all_gather x4 -> x0, blocking collectives: 64.8 us -> none  [summed_rows(): return lax.all_gather(own_rows, axis, axis=0, tiled=True)]
    all_to_all x4 -> x0, waiting for transfers between devices: 33.7 us -> none  [summed_rows(): parts = lax.all_to_all(shard, axis, 0, 0, tiled=True)]
    all_to_all x4 -> x0, starting transfers between devices: 27.6 us -> none  [summed_rows(): parts = lax.all_to_all(shard, axis, 0, 0, tiled=True)]
    ppermute x8, waiting for transfers between devices: 16.1 us -> 31.1 us  [from_partner(): lax.ppermute(shard, axis, [(i, i ^ 1 << stride) for i in range(lax.axis_s...]
  transfers between devices with their start and end apart: 14 -> 26, of which waited for: 9 -> 21; matrix products, arithmetic and copies ran while one was open for 39% -> 34% of each run, Pallas kernels for 0% -> 0%
where the time goes in v5:
time: 487 us; the launch traced here: 480 us
  other arithmetic  197 us (40%)
  waiting for transfers between devices  132 us (27%)
  blocking collectives  82.4 us (17%)
  matrix products  38.1 us (8%)
  starting transfers between devices  25.3 us (5%)
    ppermute x16, waiting for transfers between devices, summed_rows(): other = lax.ppermute(own_rows, axis, [(i, i ^ step) for i in range(count)])  97.9 us
    all_to_all x4, blocking collectives, summed_rows(): parts = lax.all_to_all(shard, axis, 0, 0, tiled=True)  82.4 us
    another operation x12, other arithmetic, rotation_of(): lax.linalg.cholesky(normal[half:, half:] - highest_dot(low_21, low_21.T),...  49.6 us
    another operation x12, other arithmetic, rotation_of(): low_11 = lax.linalg.cholesky(normal[:half, :half], symmetrize_input=False)  49.6 us
    another operation x8, other arithmetic, rotation_of(): jax.scipy.linalg.solve_triangular(low_22, mixed_cols[:, half:].T - highes...  42.7 us
    another operation x8, other arithmetic, rotation_of(): jax.scipy.linalg.solve_triangular(low_11, mixed_cols[:, :half].T, lower=T...  41.9 us
    ppermute x8, waiting for transfers between devices, from_partner(): lax.ppermute(shard, axis, [(i, i ^ 1 << stride) for i in range(lax.axis_s...  31.1 us
    dot_general x7, matrix products, rotated(): jnp.dot(rotation, stacked, preferred_element_type=jnp.float32)  17.9 us
  transfers between devices with their start and end apart: 26, of which 21 were waited for; matrix products, arithmetic and copies ran while one was open for 34% of the time, Pallas kernels for 0%

profile of v5, /device:TPU:1, one launch (start us, length us, event | category | flops | bytes accessed | tf_op | source)
XLA Modules:
  0.0 479.5 jit_solution(14994409652265501165)
XLA Ops:
  26.4 20.8 %all_to_all.36 = bf16[16,32,256]{2,1,0:T(8,128)(2,1)S(1)} all-to-all(bf16[16,32,256]{2,1,0:T(8,128)(2,1)S(1)} %bitcast.172), channel_id=1, replica_groups=mesh['tm'=16,'space'=16] {'space'}, dimensions={0} | all-to-all | bytes 524288 | tf_op jit(solution)/shard_map/all_to_all | solution.py:15
  52.3 9.2 %collective-permute-done.6 = f32[128,256]{1,0:T(8,128)} collective-permute-done((f32[128,256]{1,0:T(8,128)S(1)}, f32[128,256]{1,0:T(8,128)}, u32[]{:S(2)}, u32[]{:S(2)}) %collective-permute-start.6) | collective-permute-done | bytes 131104 | tf_op jit(solution)/shard_map/ppermute | solution.py:21
  78.7 11.7 %custom-call.26 = f32[128,128]{1,0:T(8,128)S(1)} custom-call(f32[128,128]{1,0:T(8,128)S(1)} %slice.164), custom_call_target="Cholesky" | custom-call | tf_op jit(solution)/shard_map/cholesky/custom-call.1 | solution.py:87
  91.8 9.8 %custom-call.27 = f32[1,128,128]{1,2,0:T(8,128)S(1)} custom-call(f32[1,128,128]{2,1,0:T(8,128)S(1)} %fusion.39), custom_call_target="InvertDiagBlocksLowerTriangular" | custom-call | tf_op jit(solution)/shard_map/jit(_solve_triangular)/triangular_solve | solution.py:94
  102.2 11.7 %custom-call.29 = f32[128,128]{1,0:T(8,128)S(1)} custom-call(f32[128,128]{1,0:T(8,128)S(1)} %slice_subtract_fusion.5), custom_call_target="Cholesky" | custom-call | tf_op jit(solution)/shard_map/cholesky/custom-call.1 | solution.py:91
  115.2 10.0 %custom-call.30 = f32[1,128,128]{1,2,0:T(8,128)S(1)} custom-call(f32[1,128,128]{2,1,0:T(8,128)S(1)} %fusion.40), custom_call_target="InvertDiagBlocksLowerTriangular" | custom-call | tf_op jit(solution)/shard_map/jit(_solve_triangular)/triangular_solve | solution.py:95
  145.1 20.5 %all_to_all.37 = bf16[16,32,256]{2,1,0:T(8,128)(2,1)S(1)} all-to-all(bf16[16,32,256]{2,1,0:T(8,128)(2,1)S(1)} %bitcast.173), channel_id=1, replica_groups=mesh['tm'=16,'space'=16] {'space'}, dimensions={0} | all-to-all | bytes 524288 | tf_op jit(solution)/shard_map/all_to_all | solution.py:15
  183.5 10.4 %collective-permute-done.13 = f32[256,256]{1,0:T(8,128)S(1)} collective-permute-done((f32[256,256]{1,0:T(8,128)S(1)}, f32[256,256]{1,0:T(8,128)S(1)}, u32[]{:S(2)}, u32[]{:S(2)}) %collective-permute-start.13) | collective-permute-done | bytes 262176 | tf_op jit(solution)/shard_map/ppermute | solution.py:21
  195.0 11.7 %custom-call.31 = f32[128,128]{1,0:T(8,128)S(1)} custom-call(f32[128,128]{1,0:T(8,128)S(1)} %slice.171), custom_call_target="Cholesky" | custom-call | tf_op jit(solution)/shard_map/cholesky/custom-call.1 | solution.py:87
  208.1 9.8 %custom-call.32 = f32[1,128,128]{1,2,0:T(8,128)S(1)} custom-call(f32[1,128,128]{2,1,0:T(8,128)S(1)} %fusion.41), custom_call_target="InvertDiagBlocksLowerTriangular" | custom-call | tf_op jit(solution)/shard_map/jit(_solve_triangular)/triangular_solve | solution.py:94
  218.5 11.7 %custom-call.34 = f32[128,128]{1,0:T(8,128)S(1)} custom-call(f32[128,128]{1,0:T(8,128)S(1)} %slice_subtract_fusion.4), custom_call_target="Cholesky" | custom-call | tf_op jit(solution)/shard_map/cholesky/custom-call.1 | solution.py:91
  231.6 9.9 %custom-call.35 = f32[1,128,128]{1,2,0:T(8,128)S(1)} custom-call(f32[1,128,128]{2,1,0:T(8,128)S(1)} %fusion.42), custom_call_target="InvertDiagBlocksLowerTriangular" | custom-call | tf_op jit(solution)/shard_map/jit(_solve_triangular)/triangular_solve | solution.py:95
  246.8 9.5 %collective-permute-done.14 = bf16[256,512]{1,0:T(8,128)(2,1)S(1)} collective-permute-done((bf16[256,512]{1,0:T(8,128)(2,1)S(1)}, bf16[256,512]{1,0:T(8,128)(2,1)S(1)}, u32[]{:S(2)}, u32[]{:S(2)}) %collective-permute-start.14) | collective-permute-done | bytes 262176 | tf_op jit(solution)/shard_map/ppermute | solution.py:49
  261.2 20.5 %all_to_all.38 = bf16[16,32,256]{2,1,0:T(8,128)(2,1)S(1)} all-to-all(bf16[16,32,256]{2,1,0:T(8,128)(2,1)S(1)} %bitcast.174), channel_id=1, replica_groups=mesh['tm'=16,'space'=16] {'space'}, dimensions={0} | all-to-all | bytes 524288 | tf_op jit(solution)/shard_map/all_to_all | solution.py:15
  311.1 11.7 %custom-call.36 = f32[128,128]{1,0:T(8,128)S(1)} custom-call(f32[128,128]{1,0:T(8,128)S(1)} %slice.178), custom_call_target="Cholesky" | custom-call | tf_op jit(solution)/shard_map/cholesky/custom-call.1 | solution.py:87
  324.2 9.8 %custom-call.37 = f32[1,128,128]{1,2,0:T(8,128)S(1)} custom-call(f32[1,128,128]{2,1,0:T(8,128)S(1)} %fusion.43), custom_call_target="InvertDiagBlocksLowerTriangular" | custom-call | tf_op jit(solution)/shard_map/jit(_solve_triangular)/triangular_solve | solution.py:94
  334.6 11.7 %custom-call.39 = f32[128,128]{1,0:T(8,128)S(1)} custom-call(f32[128,128]{1,0:T(8,128)S(1)} %slice_subtract_fusion.3), custom_call_target="Cholesky" | custom-call | tf_op jit(solution)/shard_map/cholesky/custom-call.1 | solution.py:91
  347.6 10.2 %custom-call.40 = f32[1,128,128]{1,2,0:T(8,128)S(1)} custom-call(f32[1,128,128]{2,1,0:T(8,128)S(1)} %fusion.44), custom_call_target="InvertDiagBlocksLowerTriangular" | custom-call | tf_op jit(solution)/shard_map/jit(_solve_triangular)/triangular_solve | solution.py:95
  378.6 20.5 %all_to_all.39 = bf16[16,32,256]{2,1,0:T(8,128)(2,1)S(1)} all-to-all(bf16[16,32,256]{2,1,0:T(8,128)(2,1)S(1)} %bitcast.175), channel_id=1, replica_groups=mesh['tm'=16,'space'=16] {'space'}, dimensions={0} | all-to-all | bytes 524288 | tf_op jit(solution)/shard_map/all_to_all | solution.py:15
  413.6 14.0 %collective-permute-done.25 = f32[256,256]{1,0:T(8,128)S(1)} collective-permute-done((f32[256,256]{1,0:T(8,128)S(1)}, f32[256,256]{1,0:T(8,128)S(1)}, u32[]{:S(2)}, u32[]{:S(2)}) %collective-permute-start.25) | collective-permute-done | bytes 262176 | tf_op jit(solution)/shard_map/ppermute | solution.py:21
  428.7 11.7 %custom-call.41 = f32[128,128]{1,0:T(8,128)S(1)} custom-call(f32[128,128]{1,0:T(8,128)S(1)} %slice.185), custom_call_target="Cholesky" | custom-call | tf_op jit(solution)/shard_map/cholesky/custom-call.1 | solution.py:87
  441.8 9.8 %custom-call.42 = f32[1,128,128]{1,2,0:T(8,128)S(1)} custom-call(f32[1,128,128]{2,1,0:T(8,128)S(1)} %fusion.45), custom_call_target="InvertDiagBlocksLowerTriangular" | custom-call | tf_op jit(solution)/shard_map/jit(_solve_triangular)/triangular_solve | solution.py:94
  452.6 11.7 %custom-call.44 = f32[128,128]{1,0:T(8,128)S(1)} custom-call(f32[128,128]{1,0:T(8,128)S(1)} %slice_subtract_fusion.2), custom_call_target="Cholesky" | custom-call | tf_op jit(solution)/shard_map/cholesky/custom-call.1 | solution.py:91
  465.6 10.0 %custom-call.45 = f32[1,128,128]{1,2,0:T(8,128)S(1)} custom-call(f32[1,128,128]{2,1,0:T(8,128)S(1)} %fusion.46), custom_call_target="InvertDiagBlocksLowerTriangular" | custom-call | tf_op jit(solution)/shard_map/jit(_solve_triangular)/triangular_solve | solution.py:95
  (180 shorter events, 179.8 us)
Async XLA Ops:
  6.1 17.1 %collective-permute-start.2 = (bf16[256,8,128]{0,2,1:T(8,128)(2,1)S(1)}, bf16[256,8,128]{0,2,1:T(8,128)(2,1)S(1)}, u32[]{:S(2)}, u32[]{:S(2)}) collective-permute-start(bf16[256,8,128]{0,2,1:T(8,128)(2,1)S(1)} %multiply_convert_fusion), channel_id=1, source_target_pairs={{0,16},{16,0},{32,48},{48,32},{64,80},{80,64},{96,112},{112,96},{1... | collective-permute-start | bytes 1572872 | tf_op jit(solution)/shard_map/ppermute | solution.py:49
  8.2 7.2 %collective-permute-start = (bf16[256,1,128]{0,2,1:T(8,128)(2,1)S(1)}, bf16[256,1,128]{0,2,1:T(8,128)(2,1)S(1)}, u32[]{:S(2)}, u32[]{:S(2)}) collective-permute-start(bf16[256,1,128]{0,2,1:T(8,128)(2,1)S(1)} %get-tuple-element.6), channel_id=1, source_target_pairs={{0,1},{1,2},{2,3},{3,4},{4,5},{5,6},{6,7},{7,8},{8,9},{9,10},{10,1... | collective-permute-start | bytes 196616 | tf_op jit(solution)/shard_map/ppermute | solution.py:39
  12.6 5.9 %collective-permute-start.1 = (bf16[256,1,128]{0,2,1:T(8,128)(2,1)S(1)}, bf16[256,1,128]{0,2,1:T(8,128)(2,1)S(1)}, u32[]{:S(2)}, u32[]{:S(2)}) collective-permute-start(bf16[256,1,128]{0,2,1:T(8,128)(2,1)S(1)} %get-tuple-element.8), channel_id=1, source_target_pairs={{1,0},{2,1},{3,2},{4,3},{5,4},{6,5},{7,6},{8,7},{9,8},{10,9},{11,1... | collective-permute-start | bytes 196616 | tf_op jit(solution)/shard_map/ppermute | solution.py:41
  18.5 4.7 collective-permute-start.3
  47.2 1.3 collective-permute-start.4
  48.5 3.6 collective-permute-start.5
  52.2 9.3 %collective-permute-start.6 = (f32[128,256]{1,0:T(8,128)S(1)}, f32[128,256]{1,0:T(8,128)}, u32[]{:S(2)}, u32[]{:S(2)}) collective-permute-start(f32[128,256]{1,0:T(8,128)S(1)} %maximum_select_fusion.8), channel_id=1, source_target_pairs={{0,4},{1,5},{2,6},{3,7},{4,0},{5,1},{6,2},{7,3},{8,12},{9,13},{10,... | collective-permute-start | bytes 393224 | tf_op jit(solution)/shard_map/ppermute | solution.py:21
  62.5 14.1 %collective-permute-start.7 = (f32[256,256]{1,0:T(8,128)S(1)}, f32[256,256]{1,0:T(8,128)}, u32[]{:S(2)}, u32[]{:S(2)}) collective-permute-start(f32[256,256]{1,0:T(8,128)S(1)} %maximum_select_fusion.4), channel_id=1, source_target_pairs={{0,8},{1,9},{2,10},{3,11},{4,12},{5,13},{6,14},{7,15},{8,0},{9,1},... | collective-permute-start | bytes 786440 | tf_op jit(solution)/shard_map/ppermute | solution.py:21
  64.5 75.8 %collective-permute-start.9 = (bf16[512,3072]{0,1:T(8,128)(2,1)}, bf16[512,3072]{0,1:T(8,128)(2,1)}, u32[]{:S(2)}, u32[]{:S(2)}) collective-permute-start(bf16[512,3072]{0,1:T(8,128)(2,1)} %pad_maximum_fusion), channel_id=1, source_target_pairs={{0,32},{16,48},{32,0},{48,16},{64,96},{80,112},{96,64},{112,80},{1... | collective-permute-start | bytes 9437192 | tf_op jit(solution)/shard_map/ppermute | solution.py:49
  126.7 13.6 %collective-permute-start.8 = (bf16[256,512]{1,0:T(8,128)(2,1)S(1)}, bf16[256,512]{1,0:T(8,128)(2,1)S(1)}, u32[]{:S(2)}, u32[]{:S(2)}) collective-permute-start(bf16[256,512]{1,0:T(8,128)(2,1)S(1)} %fusion.20), channel_id=1, source_target_pairs={{0,32},{16,48},{32,0},{48,16},{64,96},{80,112},{96,64},{112,80},{1... | collective-permute-start | bytes 786440 | tf_op jit(solution)/shard_map/ppermute | solution.py:49
  165.7 1.3 collective-permute-start.10
  167.0 3.6 collective-permute-start.11
  170.6 9.2 %collective-permute-start.12 = (f32[128,256]{1,0:T(8,128)S(1)}, f32[128,256]{1,0:T(8,128)S(1)}, u32[]{:S(2)}, u32[]{:S(2)}) collective-permute-start(f32[128,256]{1,0:T(8,128)S(1)} %maximum_select_fusion.9), channel_id=1, source_target_pairs={{0,4},{1,5},{2,6},{3,7},{4,0},{5,1},{6,2},{7,3},{8,12},{9,13},{10,... | collective-permute-start | bytes 393224 | tf_op jit(solution)/shard_map/ppermute | solution.py:21
  179.9 14.1 %collective-permute-start.13 = (f32[256,256]{1,0:T(8,128)S(1)}, f32[256,256]{1,0:T(8,128)S(1)}, u32[]{:S(2)}, u32[]{:S(2)}) collective-permute-start(f32[256,256]{1,0:T(8,128)S(1)} %maximum_select_fusion.5), channel_id=1, source_target_pairs={{0,8},{1,9},{2,10},{3,11},{4,12},{5,13},{6,14},{7,15},{8,0},{9,1},... | collective-permute-start | bytes 786440 | tf_op jit(solution)/shard_map/ppermute | solution.py:21
  181.9 74.5 %collective-permute-start.15 = (bf16[512,3072]{1,0:T(8,128)(2,1)}, bf16[512,3072]{1,0:T(8,128)(2,1)}, u32[]{:S(2)}, u32[]{:S(2)}) collective-permute-start(bf16[512,3072]{1,0:T(8,128)(2,1)} %pad_maximum_fusion.1), channel_id=1, source_target_pairs={{0,64},{16,80},{32,96},{48,112},{64,0},{80,16},{96,32},{112,48},{1... | collective-permute-start | bytes 9437192 | tf_op jit(solution)/shard_map/ppermute | solution.py:49
  243.0 13.3 %collective-permute-start.14 = (bf16[256,512]{1,0:T(8,128)(2,1)S(1)}, bf16[256,512]{1,0:T(8,128)(2,1)S(1)}, u32[]{:S(2)}, u32[]{:S(2)}) collective-permute-start(bf16[256,512]{1,0:T(8,128)(2,1)S(1)} %fusion.21), channel_id=1, source_target_pairs={{0,64},{16,80},{32,96},{48,112},{64,0},{80,16},{96,32},{112,48},{1... | collective-permute-start | bytes 786440 | tf_op jit(solution)/shard_map/ppermute | solution.py:49
  283.1 3.6 collective-permute-start.17
  286.7 9.2 %collective-permute-start.18 = (f32[128,256]{1,0:T(8,128)S(1)}, f32[128,256]{1,0:T(8,128)S(1)}, u32[]{:S(2)}, u32[]{:S(2)}) collective-permute-start(f32[128,256]{1,0:T(8,128)S(1)} %maximum_select_fusion.10), channel_id=1, source_target_pairs={{0,4},{1,5},{2,6},{3,7},{4,0},{5,1},{6,2},{7,3},{8,12},{9,13},{10,... | collective-permute-start | bytes 393224 | tf_op jit(solution)/shard_map/ppermute | solution.py:21
  296.0 14.1 %collective-permute-start.19 = (f32[256,256]{1,0:T(8,128)S(1)}, f32[256,256]{1,0:T(8,128)S(1)}, u32[]{:S(2)}, u32[]{:S(2)}) collective-permute-start(f32[256,256]{1,0:T(8,128)S(1)} %maximum_select_fusion.6), channel_id=1, source_target_pairs={{0,8},{1,9},{2,10},{3,11},{4,12},{5,13},{6,14},{7,15},{8,0},{9,1},... | collective-permute-start | bytes 786440 | tf_op jit(solution)/shard_map/ppermute | solution.py:21
  297.9 75.8 %collective-permute-start.21 = (bf16[512,3072]{1,0:T(8,128)(2,1)}, bf16[512,3072]{1,0:T(8,128)(2,1)}, u32[]{:S(2)}, u32[]{:S(2)}) collective-permute-start(bf16[512,3072]{1,0:T(8,128)(2,1)} %pad_maximum_fusion.2), channel_id=1, source_target_pairs={{0,128},{16,144},{32,160},{48,176},{64,192},{80,208},{96,224},{112... | collective-permute-start | bytes 9437192 | tf_op jit(solution)/shard_map/ppermute | solution.py:49
  359.3 14.4 %collective-permute-start.20 = (bf16[256,512]{1,0:T(8,128)(2,1)S(1)}, bf16[256,512]{1,0:T(8,128)(2,1)S(1)}, u32[]{:S(2)}, u32[]{:S(2)}) collective-permute-start(bf16[256,512]{1,0:T(8,128)(2,1)S(1)} %fusion.22), channel_id=1, source_target_pairs={{0,128},{16,144},{32,160},{48,176},{64,192},{80,208},{96,224},{112... | collective-permute-start | bytes 786440 | tf_op jit(solution)/shard_map/ppermute | solution.py:49
  400.5 3.6 collective-permute-start.23
  404.1 9.2 %collective-permute-start.24 = (f32[128,256]{1,0:T(8,128)S(1)}, f32[128,256]{1,0:T(8,128)S(1)}, u32[]{:S(2)}, u32[]{:S(2)}) collective-permute-start(f32[128,256]{1,0:T(8,128)S(1)} %maximum_select_fusion.11), channel_id=1, source_target_pairs={{0,4},{1,5},{2,6},{3,7},{4,0},{5,1},{6,2},{7,3},{8,12},{9,13},{10,... | collective-permute-start | bytes 393224 | tf_op jit(solution)/shard_map/ppermute | solution.py:21
  413.4 14.3 %collective-permute-start.25 = (f32[256,256]{1,0:T(8,128)S(1)}, f32[256,256]{1,0:T(8,128)S(1)}, u32[]{:S(2)}, u32[]{:S(2)}) collective-permute-start(f32[256,256]{1,0:T(8,128)S(1)} %maximum_select_fusion.7), channel_id=1, source_target_pairs={{0,8},{1,9},{2,10},{3,11},{4,12},{5,13},{6,14},{7,15},{8,0},{9,1},... | collective-permute-start | bytes 786440 | tf_op jit(solution)/shard_map/ppermute | solution.py:21
  (8 other events, 181.6 us)

commit v6 on v3

--- a/solution.py
+++ b/solution.py
@@ -103,7 +103,11 @@
     mean_state = jnp.mean(stored[0].astype(jnp.float32), axis=0)
     picked = jnp.take(stored[0], snapshot[0], axis=0)
     anomaly = ((picked.astype(jnp.float32) - mean_state) * sea_float).astype(jnp.bfloat16)
-    other_anomaly = from_partner(anomaly, "tm", 0)
+    other_picked = from_partner(picked, "tm", 0)
+    other_mean = from_partner(mean_state, "tm", 0)
+    other_anomaly = ((other_picked.astype(jnp.float32) - other_mean) * sea_float).astype(
+        jnp.bfloat16
+    )
     padded = with_halo(anomaly, (("space", 1),), 1)
     basis_now = balance(padded, balance_coef, sea_float)
     levels = lax.axis_size("tm").bit_length() - 1

time: 414 us -> 422 us (1.019)
  waiting for transfers between devices: 52.9 us -> 59 us
    ppermute x8 -> x9, waiting for transfers between devices: 16.1 us -> 22.2 us  [from_partner(): lax.ppermute(shard, axis, [(i, i ^ 1 << stride) for i in range(lax.axis_s...]
    ppermute x8 -> x9, starting transfers between devices: 16.6 us -> 16.3 us  [from_partner(): lax.ppermute(shard, axis, [(i, i ^ 1 << stride) for i in range(lax.axis_s...]
  transfers between devices with their start and end apart: 14 -> 15, of which waited for: 9 -> 9; matrix products, arithmetic and copies ran while one was open for 39% -> 40% of each run, Pallas kernels for 0% -> 0%
where the time goes in v6:
time: 422 us; the launch traced here: 416 us
  other arithmetic  199 us (47%)
  blocking collectives  64.8 us (15%)
  waiting for transfers between devices  59 us (14%)
  starting transfers between devices  51.2 us (12%)
  matrix products  38.1 us (9%)
    all_gather x4, blocking collectives, summed_rows(): return lax.all_gather(own_rows, axis, axis=0, tiled=True)  64.8 us
    another operation x12, other arithmetic, rotation_of(): low_11 = lax.linalg.cholesky(normal[:half, :half], symmetrize_input=False)  49.6 us
    another operation x12, other arithmetic, rotation_of(): lax.linalg.cholesky(normal[half:, half:] - highest_dot(low_21, low_21.T),...  49.6 us
    another operation x8, other arithmetic, rotation_of(): jax.scipy.linalg.solve_triangular(low_22, mixed_cols[:, half:].T - highes...  42.8 us
    another operation x8, other arithmetic, rotation_of(): jax.scipy.linalg.solve_triangular(low_11, mixed_cols[:, :half].T, lower=T...  41.9 us
    all_to_all x4, waiting for transfers between devices, summed_rows(): parts = lax.all_to_all(shard, axis, 0, 0, tiled=True)  34.1 us
    all_to_all x4, starting transfers between devices, summed_rows(): parts = lax.all_to_all(shard, axis, 0, 0, tiled=True)  28.5 us
    ppermute x9, waiting for transfers between devices, from_partner(): lax.ppermute(shard, axis, [(i, i ^ 1 << stride) for i in range(lax.axis_s...  22.2 us
  transfers between devices with their start and end apart: 15, of which 9 were waited for; matrix products, arithmetic and copies ran while one was open for 40% of the time, Pallas kernels for 0%

profile of v6, /device:TPU:1, one launch (start us, length us, event | category | flops | bytes accessed | tf_op | source)
XLA Modules:
  0.0 415.9 jit_solution(7245602516053465394)
XLA Ops:
  18.9 10.0 %collective-permute-done.4 = bf16[256,2,128]{0,2,1:T(8,128)(2,1)S(1)} collective-permute-done((bf16[256,2,128]{0,2,1:T(8,128)(2,1)S(1)}, bf16[256,2,128]{0,2,1:T(8,128)(2,1)S(1)}, u32[]{:S(2)}, u32[]{:S(2)}) %collective-permute-start.4) | collective-permute-done | bytes 131104 | tf_op jit(solution)/shard_map/ppermute | solution.py:39
  33.6 10.3 %all-to-all-start = ((bf16[16,32,256]{2,1,0:T(8,128)(2,1)}), bf16[16,32,256]{2,1,0:T(8,128)(2,1)S(1)}, u32[]{:S(2)}, u32[]{:S(2)}) async-start(bf16[16,32,256]{2,1,0:T(8,128)(2,1)} %bitcast.13), calls=%async_computation | async-start | bytes 524288 | tf_op jit(solution)/shard_map/all_to_all | solution.py:15
  55.6 16.4 %all_gather.12 = f32[512,256]{1,0:T(8,128)S(1)} all-gather(f32[32,256]{1,0:T(8,128)S(1)} %convert_reduce_fusion.4), channel_id=1, replica_groups=mesh['tm'=16,'space'=16] {'space'}, dimensions={0}, use_global_device_ids=true | all-gather | bytes 557056 | tf_op jit(solution)/shard_map/all_gather | solution.py:18
  73.1 11.7 %custom-call.26 = f32[128,128]{1,0:T(8,128)S(1)} custom-call(f32[128,128]{1,0:T(8,128)S(1)} %slice.164), custom_call_target="Cholesky" | custom-call | tf_op jit(solution)/shard_map/cholesky/custom-call.1 | solution.py:77
  86.1 9.8 %custom-call.27 = f32[1,128,128]{1,2,0:T(8,128)S(1)} custom-call(f32[1,128,128]{2,1,0:T(8,128)S(1)} %fusion.27), custom_call_target="InvertDiagBlocksLowerTriangular" | custom-call | tf_op jit(solution)/shard_map/jit(_solve_triangular)/triangular_solve | solution.py:84
  96.5 11.7 %custom-call.29 = f32[128,128]{1,0:T(8,128)S(1)} custom-call(f32[128,128]{1,0:T(8,128)S(1)} %convolution_subtract_fusion.7), custom_call_target="Cholesky" | custom-call | tf_op jit(solution)/shard_map/cholesky/custom-call.1 | solution.py:81
  109.6 9.9 %custom-call.30 = f32[1,128,128]{1,2,0:T(8,128)S(1)} custom-call(f32[1,128,128]{2,1,0:T(8,128)S(1)} %fusion.28), custom_call_target="InvertDiagBlocksLowerTriangular" | custom-call | tf_op jit(solution)/shard_map/jit(_solve_triangular)/triangular_solve | solution.py:85
  145.0 8.4 %all-to-all-done.1 = bf16[16,32,256]{2,1,0:T(8,128)(2,1)S(1)} async-done(((bf16[16,32,256]{2,1,0:T(8,128)(2,1)}), bf16[16,32,256]{2,1,0:T(8,128)(2,1)S(1)}, u32[]{:S(2)}, u32[]{:S(2)}) %all-to-all-start.1) | async-done | bytes 262176 | tf_op jit(solution)/shard_map/all_to_all | solution.py:15
  153.5 16.1 %all_gather.13 = f32[512,256]{1,0:T(8,128)S(1)} all-gather(f32[32,256]{1,0:T(8,128)S(1)} %convert_reduce_fusion.3), channel_id=1, replica_groups=mesh['tm'=16,'space'=16] {'space'}, dimensions={0}, use_global_device_ids=true | all-gather | bytes 557056 | tf_op jit(solution)/shard_map/all_gather | solution.py:18
  170.7 11.7 %custom-call.31 = f32[128,128]{1,0:T(8,128)S(1)} custom-call(f32[128,128]{1,0:T(8,128)S(1)} %slice.171), custom_call_target="Cholesky" | custom-call | tf_op jit(solution)/shard_map/cholesky/custom-call.1 | solution.py:77
  183.7 9.8 %custom-call.32 = f32[1,128,128]{1,2,0:T(8,128)S(1)} custom-call(f32[1,128,128]{2,1,0:T(8,128)S(1)} %fusion.29), custom_call_target="InvertDiagBlocksLowerTriangular" | custom-call | tf_op jit(solution)/shard_map/jit(_solve_triangular)/triangular_solve | solution.py:84
  194.1 11.7 %custom-call.34 = f32[128,128]{1,0:T(8,128)S(1)} custom-call(f32[128,128]{1,0:T(8,128)S(1)} %convolution_subtract_fusion.6), custom_call_target="Cholesky" | custom-call | tf_op jit(solution)/shard_map/cholesky/custom-call.1 | solution.py:81
  207.2 10.2 %custom-call.35 = f32[1,128,128]{1,2,0:T(8,128)S(1)} custom-call(f32[1,128,128]{2,1,0:T(8,128)S(1)} %fusion.30), custom_call_target="InvertDiagBlocksLowerTriangular" | custom-call | tf_op jit(solution)/shard_map/jit(_solve_triangular)/triangular_solve | solution.py:85
  249.9 16.1 %all_gather.14 = f32[512,256]{1,0:T(8,128)S(1)} all-gather(f32[32,256]{1,0:T(8,128)S(1)} %convert_reduce_fusion.2), channel_id=1, replica_groups=mesh['tm'=16,'space'=16] {'space'}, dimensions={0}, use_global_device_ids=true | all-gather | bytes 557056 | tf_op jit(solution)/shard_map/all_gather | solution.py:18
  267.0 11.7 %custom-call.36 = f32[128,128]{1,0:T(8,128)S(1)} custom-call(f32[128,128]{1,0:T(8,128)S(1)} %slice.178), custom_call_target="Cholesky" | custom-call | tf_op jit(solution)/shard_map/cholesky/custom-call.1 | solution.py:77
  280.1 9.8 %custom-call.37 = f32[1,128,128]{1,2,0:T(8,128)S(1)} custom-call(f32[1,128,128]{2,1,0:T(8,128)S(1)} %fusion.31), custom_call_target="InvertDiagBlocksLowerTriangular" | custom-call | tf_op jit(solution)/shard_map/jit(_solve_triangular)/triangular_solve | solution.py:84
  290.5 11.7 %custom-call.39 = f32[128,128]{1,0:T(8,128)S(1)} custom-call(f32[128,128]{1,0:T(8,128)S(1)} %convolution_subtract_fusion.5), custom_call_target="Cholesky" | custom-call | tf_op jit(solution)/shard_map/cholesky/custom-call.1 | solution.py:81
  303.5 10.0 %custom-call.40 = f32[1,128,128]{1,2,0:T(8,128)S(1)} custom-call(f32[1,128,128]{2,1,0:T(8,128)S(1)} %fusion.32), custom_call_target="InvertDiagBlocksLowerTriangular" | custom-call | tf_op jit(solution)/shard_map/jit(_solve_triangular)/triangular_solve | solution.py:85
  335.9 11.6 %all-to-all-done.3 = bf16[16,32,256]{2,1,0:T(8,128)(2,1)S(1)} async-done(((bf16[16,32,256]{2,1,0:T(8,128)(2,1)}), bf16[16,32,256]{2,1,0:T(8,128)(2,1)S(1)}, u32[]{:S(2)}, u32[]{:S(2)}) %all-to-all-start.3) | async-done | bytes 262176 | tf_op jit(solution)/shard_map/all_to_all | solution.py:15
  347.5 16.2 %all_gather.15 = f32[512,256]{1,0:T(8,128)S(1)} all-gather(f32[32,256]{1,0:T(8,128)S(1)} %convert_reduce_fusion.1), channel_id=1, replica_groups=mesh['tm'=16,'space'=16] {'space'}, dimensions={0}, use_global_device_ids=true | all-gather | bytes 557056 | tf_op jit(solution)/shard_map/all_gather | solution.py:18
  364.7 11.7 %custom-call.41 = f32[128,128]{1,0:T(8,128)S(1)} custom-call(f32[128,128]{1,0:T(8,128)S(1)} %slice.185), custom_call_target="Cholesky" | custom-call | tf_op jit(solution)/shard_map/cholesky/custom-call.1 | solution.py:77
  377.8 9.8 %custom-call.42 = f32[1,128,128]{1,2,0:T(8,128)S(1)} custom-call(f32[1,128,128]{2,1,0:T(8,128)S(1)} %fusion.33), custom_call_target="InvertDiagBlocksLowerTriangular" | custom-call | tf_op jit(solution)/shard_map/jit(_solve_triangular)/triangular_solve | solution.py:84
  388.6 11.7 %custom-call.44 = f32[128,128]{1,0:T(8,128)S(1)} custom-call(f32[128,128]{1,0:T(8,128)S(1)} %convolution_subtract_fusion.4), custom_call_target="Cholesky" | custom-call | tf_op jit(solution)/shard_map/cholesky/custom-call.1 | solution.py:81
  401.7 10.1 %custom-call.45 = f32[1,128,128]{1,2,0:T(8,128)S(1)} custom-call(f32[1,128,128]{2,1,0:T(8,128)S(1)} %fusion.34), custom_call_target="InvertDiagBlocksLowerTriangular" | custom-call | tf_op jit(solution)/shard_map/jit(_solve_triangular)/triangular_solve | solution.py:85
  (144 shorter events, 136.4 us)
Async XLA Ops:
  0.0 15.3 %copy-start.3 = (s32[8,128]{1,0:T(8,128)S(1)}, s32[8,128]{1,0:T(8,128)}, u32[]{:S(2)}) copy-start(s32[8,128]{1,0:T(8,128)} %param.12) | copy-start | bytes 12292
  0.0 15.3 %copy-start.4 = (f32[8,128]{1,0:T(8,128)S(1)}, f32[8,128]{1,0:T(8,128)}, u32[]{:S(2)}) copy-start(f32[8,128]{1,0:T(8,128)} %param.11) | copy-start | bytes 12292
  1.4 27.6 %collective-permute-start.3 = (f32[8,128]{1,0:T(8,128)S(1)}, f32[8,128]{1,0:T(8,128)S(1)}, u32[]{:S(2)}, u32[]{:S(2)}) collective-permute-start(f32[8,128]{1,0:T(8,128)S(1)} %broadcast_multiply_fusion), channel_id=1, source_target_pairs={{0,16},{16,0},{32,48},{48,32},{64,80},{80,64},{96,112},{112,96},{1... | collective-permute-start | bytes 12296 | tf_op jit(solution)/shard_map/ppermute | solution.py:39
  8.2 7.5 %collective-permute-start = (bf16[256,1,128]{0,2,1:T(8,128)(2,1)S(1)}, bf16[256,1,128]{0,2,1:T(8,128)(2,1)S(1)}, u32[]{:S(2)}, u32[]{:S(2)}) collective-permute-start(bf16[256,1,128]{0,2,1:T(8,128)(2,1)S(1)} %get-tuple-element.10), channel_id=1, source_target_pairs={{0,1},{1,2},{2,3},{3,4},{4,5},{5,6},{6,7},{7,8},{8,9},{9,10},{10,1... | collective-permute-start | bytes 196616 | tf_op jit(solution)/shard_map/ppermute | solution.py:29
  12.6 5.9 %collective-permute-start.1 = (bf16[256,1,128]{0,2,1:T(8,128)(2,1)S(1)}, bf16[256,1,128]{0,2,1:T(8,128)(2,1)S(1)}, u32[]{:S(2)}, u32[]{:S(2)}) collective-permute-start(bf16[256,1,128]{0,2,1:T(8,128)(2,1)S(1)} %get-tuple-element.11), channel_id=1, source_target_pairs={{1,0},{2,1},{3,2},{4,3},{5,4},{6,5},{7,6},{8,7},{9,8},{10,9},{11,1... | collective-permute-start | bytes 196616 | tf_op jit(solution)/shard_map/ppermute | solution.py:31
  14.5 14.5 %collective-permute-start.2 = (bf16[256,8,128]{0,2,1:T(8,128)(2,1)S(1)}, bf16[256,8,128]{0,2,1:T(8,128)(2,1)S(1)}, u32[]{:S(2)}, u32[]{:S(2)}) collective-permute-start(bf16[256,8,128]{0,2,1:T(8,128)(2,1)S(1)} %get-tuple-element.8), channel_id=1, source_target_pairs={{0,16},{16,0},{32,48},{48,32},{64,80},{80,64},{96,112},{112,96},{1... | collective-permute-start | bytes 1572872 | tf_op jit(solution)/shard_map/ppermute | solution.py:39
  18.5 10.5 %collective-permute-start.4 = (bf16[256,2,128]{0,2,1:T(8,128)(2,1)S(1)}, bf16[256,2,128]{0,2,1:T(8,128)(2,1)S(1)}, u32[]{:S(2)}, u32[]{:S(2)}) collective-permute-start(bf16[256,2,128]{0,2,1:T(8,128)(2,1)S(1)} %pad_maximum_fusion.10), channel_id=1, source_target_pairs={{0,16},{16,0},{32,48},{48,32},{64,80},{80,64},{96,112},{112,96},{1... | collective-permute-start | bytes 393224 | tf_op jit(solution)/shard_map/ppermute | solution.py:39
  31.0 12.9 %copy-start = (bf16[256,3,8,128]{0,3,2,1:T(8,128)(2,1)}, bf16[256,3,8,128]{0,3,2,1:T(8,128)(2,1)S(1)}, u32[]{:S(2)}) copy-start(bf16[256,3,8,128]{0,3,2,1:T(8,128)(2,1)S(1)} %get-tuple-element.19) | copy-start | bytes 4718596
  33.6 21.9 %all-to-all-start = ((bf16[16,32,256]{2,1,0:T(8,128)(2,1)}), bf16[16,32,256]{2,1,0:T(8,128)(2,1)S(1)}, u32[]{:S(2)}, u32[]{:S(2)}) async-start(bf16[16,32,256]{2,1,0:T(8,128)(2,1)} %bitcast.13), calls=%async_computation | async-start | bytes 524288 | tf_op jit(solution)/shard_map/all_to_all | solution.py:15
  45.9 84.4 %collective-permute-start.6 = (bf16[512,3072]{0,1:T(8,128)(2,1)}, bf16[512,3072]{0,1:T(8,128)(2,1)}, u32[]{:S(2)}, u32[]{:S(2)}) collective-permute-start(bf16[512,3072]{0,1:T(8,128)(2,1)} %pad_maximum_fusion), channel_id=1, source_target_pairs={{0,32},{16,48},{32,0},{48,16},{64,96},{80,112},{96,64},{112,80},{1... | collective-permute-start | bytes 9437192 | tf_op jit(solution)/shard_map/ppermute | solution.py:39
  121.0 9.3 %collective-permute-start.5 = (bf16[256,512]{1,0:T(8,128)(2,1)S(1)}, bf16[256,512]{1,0:T(8,128)(2,1)S(1)}, u32[]{:S(2)}, u32[]{:S(2)}) collective-permute-start(bf16[256,512]{1,0:T(8,128)(2,1)S(1)} %fusion.20), channel_id=1, source_target_pairs={{0,32},{16,48},{32,0},{48,16},{64,96},{80,112},{96,64},{112,80},{1... | collective-permute-start | bytes 786440 | tf_op jit(solution)/shard_map/ppermute | solution.py:39
  126.0 15.9 %copy-start.1 = (bf16[256,3072]{1,0:T(8,128)(2,1)}, bf16[256,3072]{1,0:T(8,128)(2,1)S(1)}, u32[]{:S(2)}) copy-start(bf16[256,3072]{1,0:T(8,128)(2,1)S(1)} %convolution_convert_fusion.5) | copy-start | bytes 4718596
  135.8 17.7 %all-to-all-start.1 = ((bf16[16,32,256]{2,1,0:T(8,128)(2,1)}), bf16[16,32,256]{2,1,0:T(8,128)(2,1)S(1)}, u32[]{:S(2)}, u32[]{:S(2)}) async-start(bf16[16,32,256]{2,1,0:T(8,128)(2,1)} %bitcast.23), calls=%async_computation.1 | async-start | bytes 524288 | tf_op jit(solution)/shard_map/all_to_all | solution.py:15
  143.8 82.9 %collective-permute-start.8 = (bf16[512,3072]{1,0:T(8,128)(2,1)}, bf16[512,3072]{1,0:T(8,128)(2,1)}, u32[]{:S(2)}, u32[]{:S(2)}) collective-permute-start(bf16[512,3072]{1,0:T(8,128)(2,1)} %pad_maximum_fusion.1), channel_id=1, source_target_pairs={{0,64},{16,80},{32,96},{48,112},{64,0},{80,16},{96,32},{112,48},{1... | collective-permute-start | bytes 9437192 | tf_op jit(solution)/shard_map/ppermute | solution.py:39
  218.9 7.8 %collective-permute-start.7 = (bf16[256,512]{1,0:T(8,128)(2,1)S(1)}, bf16[256,512]{1,0:T(8,128)(2,1)S(1)}, u32[]{:S(2)}, u32[]{:S(2)}) collective-permute-start(bf16[256,512]{1,0:T(8,128)(2,1)S(1)} %fusion.21), channel_id=1, source_target_pairs={{0,64},{16,80},{32,96},{48,112},{64,0},{80,16},{96,32},{112,48},{1... | collective-permute-start | bytes 786440 | tf_op jit(solution)/shard_map/ppermute | solution.py:39
  222.7 15.6 %copy-start.2 = (bf16[256,3072]{1,0:T(8,128)(2,1)}, bf16[256,3072]{1,0:T(8,128)(2,1)S(1)}, u32[]{:S(2)}) copy-start(bf16[256,3072]{1,0:T(8,128)(2,1)S(1)} %convolution_convert_fusion.3) | copy-start | bytes 4718596
  232.2 17.6 %all-to-all-start.2 = ((bf16[16,32,256]{2,1,0:T(8,128)(2,1)}), bf16[16,32,256]{2,1,0:T(8,128)(2,1)S(1)}, u32[]{:S(2)}, u32[]{:S(2)}) async-start(bf16[16,32,256]{2,1,0:T(8,128)(2,1)} %bitcast.33), calls=%async_computation.2 | async-start | bytes 524288 | tf_op jit(solution)/shard_map/all_to_all | solution.py:15
  240.1 84.2 %collective-permute-start.10 = (bf16[512,3072]{1,0:T(8,128)(2,1)}, bf16[512,3072]{1,0:T(8,128)(2,1)}, u32[]{:S(2)}, u32[]{:S(2)}) collective-permute-start(bf16[512,3072]{1,0:T(8,128)(2,1)} %pad_maximum_fusion.2), channel_id=1, source_target_pairs={{0,128},{16,144},{32,160},{48,176},{64,192},{80,208},{96,224},{112... | collective-permute-start | bytes 9437192 | tf_op jit(solution)/shard_map/ppermute | solution.py:39
  315.0 9.3 %collective-permute-start.9 = (bf16[256,512]{1,0:T(8,128)(2,1)S(1)}, bf16[256,512]{1,0:T(8,128)(2,1)S(1)}, u32[]{:S(2)}, u32[]{:S(2)}) collective-permute-start(bf16[256,512]{1,0:T(8,128)(2,1)S(1)} %fusion.22), channel_id=1, source_target_pairs={{0,128},{16,144},{32,160},{48,176},{64,192},{80,208},{96,224},{112... | collective-permute-start | bytes 786440 | tf_op jit(solution)/shard_map/ppermute | solution.py:39
  320.4 8.7 %copy-start.5 = (bf16[256,3072]{1,0:T(8,128)(2,1)}, bf16[256,3072]{1,0:T(8,128)(2,1)S(1)}, u32[]{:S(2)}) copy-start(bf16[256,3072]{1,0:T(8,128)(2,1)S(1)} %convolution_convert_fusion.1) | copy-start | bytes 4718596
  329.8 17.7 %all-to-all-start.3 = ((bf16[16,32,256]{2,1,0:T(8,128)(2,1)}), bf16[16,32,256]{2,1,0:T(8,128)(2,1)S(1)}, u32[]{:S(2)}, u32[]{:S(2)}) async-start(bf16[16,32,256]{2,1,0:T(8,128)(2,1)} %bitcast.43), calls=%async_computation.3 | async-start | bytes 524288 | tf_op jit(solution)/shard_map/all_to_all | solution.py:15
